TPU v7x, 128 devices: a whole 4x4x4 slice. The times are simulated.
128 devices in a mesh: grp: 4 (over y_lo, core), chan: 32 (over z, y_hi, x).
Axes of the slice: x: 4, y: 4 (y_hi: 2, y_lo: 2; y = y_hi * 2 + y_lo), z: 4, core: 2. Of those that a mesh axis runs over, the one named last changes fastest.
Arguments:
- voltages: bfloat16 [128, 2048, 128], P(None, ('grp', 'chan')), may hold values from -6 to 6
- model_vis: bfloat16 [128, 136, 2, 128, 128], P(('grp', 'chan')), may hold values from -1.1953125 to 1.1953125
- kernel_u: bfloat16 [128, 16, 128, 128], P(('grp', 'chan')), may hold values from -1.5 to 1.5
- kernel_v: bfloat16 [128, 16, 128, 128], P(('grp', 'chan')), may hold values from -1.5 to 1.5
- pair_slot: int32 [128, 136], P(('grp', 'chan')), may hold values from 0 to 15
- slot_block: int32 [128, 16], P(('grp', 'chan')), may hold values from 0 to 1023, as said below
- slot_count: int32 [128], P(('grp', 'chan')), may hold values from 8 to 16
Outputs:
- image: float32 [256, 2048], P('chan', 'grp')
Inputs may be any that keep to these rules, and one draw needn't show every extreme that they name: `pair_slot`: pairs whose slot is at or above the channel's slot_count are not imaged. `slot_block`: the 16 block ids of one channel are distinct.
All inputs are finite; a program needn't handle non-finite values.
Results may differ from a plain program's by a relative error of at most 0.0049.
Values may be sent and summed in bfloat16 or wider, within the bound.
No kernel may reach another device: no remote copies, remote signals or barrier semaphores. Data moves between devices by JAX's collectives and lax.ppermute only.
A program may use at most 192 MiB of HBM per device.

v0:
```python
import math

import jax
import jax.numpy as jnp
import numpy as np
from jax import lax
from jax.sharding import PartitionSpec as P

ANTENNAS = 2048
SAMPLES = 64
TILE = 128
BLOCK = 128
GRID = 4096
CROP = 2048
SLOTS = 16
ROWS = 256
TILES = 16
PAIRS = 136


TWO_PI = 2.0 * math.pi


def grid_channel(antenna_volts, model_one, kernel_u_one, kernel_v_one, slots_one, count_one):
    row_tiles, col_tiles = np.triu_indices(TILES)
    antenna_tiles = antenna_volts.reshape(TILES, TILE, 2 * SAMPLES)
    swapped = jnp.concatenate(
        [-antenna_tiles[:, :, SAMPLES:], antenna_tiles[:, :, :SAMPLES]], axis=2
    )
    row_volts = antenna_tiles[row_tiles]
    real_part = jnp.einsum(
        "kat,kbt->kab", row_volts, antenna_tiles[col_tiles], preferred_element_type=jnp.float32
    )
    imag_part = jnp.einsum(
        "kat,kbt->kab", row_volts, swapped[col_tiles], preferred_element_type=jnp.float32
    )
    gram_tiles = jnp.stack([real_part, imag_part], axis=1) / SAMPLES
    residual = (gram_tiles - model_one.astype(jnp.float32)).astype(jnp.bfloat16)
    half_grid = jnp.einsum(
        "kua,kcab->kcub", kernel_u_one[row_tiles], residual, preferred_element_type=jnp.float32
    ).astype(jnp.bfloat16)
    tile_grid = jnp.einsum(
        "kcub,kvb->kucv", half_grid, kernel_v_one[col_tiles], preferred_element_type=jnp.float32
    )
    live_mask = (slots_one < count_one).astype(jnp.float32)
    slot_onehot = (slots_one[:, None] == jnp.arange(SLOTS, dtype=jnp.int32)[None, :]).astype(
        jnp.float32
    ) * live_mask[:, None]
    slot_grids = jnp.dot(
        slot_onehot.T,
        tile_grid.reshape(PAIRS, BLOCK * 2 * BLOCK),
        precision=lax.Precision.HIGHEST,
        preferred_element_type=jnp.float32,
    )
    return slot_grids.astype(jnp.bfloat16).reshape(SLOTS, BLOCK, 2 * BLOCK)


def body(voltages, model_vis, kernel_u, kernel_v, pair_slot, slot_block, slot_count):
    local_antennas = voltages.shape[1]
    direct = voltages.reshape(voltages.shape[0], 1, local_antennas, 2 * SAMPLES)
    turned = lax.all_to_all(direct, ("grp", "chan"), split_axis=0, concat_axis=1, tiled=True)
    antenna_volts = turned.reshape(ANTENNAS, 2 * SAMPLES)
    slot_grids = grid_channel(
        antenna_volts, model_vis[0], kernel_u[0], kernel_v[0], pair_slot[0], slot_count[0]
    )
    per_side = GRID // BLOCK
    blocks_here = slot_block[0]
    offsets = jnp.arange(BLOCK, dtype=jnp.int32)
    pixel_cols = jnp.arange(CROP, dtype=jnp.int32) - CROP // 2

    def column_transform(inputs):
        grid_slot, block_id = inputs
        shifted_cols = block_id % per_side * BLOCK + offsets - GRID // 2
        phase_index = shifted_cols[:, None] * pixel_cols[None, :] % GRID
        angles = phase_index.astype(jnp.float32) * (TWO_PI / GRID)
        cosine = jnp.cos(angles)
        sine_part = jnp.sin(angles)
        dft_table = jnp.concatenate(
            [
                jnp.concatenate([cosine, sine_part], axis=1),
                jnp.concatenate([-sine_part, cosine], axis=1),
            ],
            axis=0,
        )
        return jnp.dot(
            grid_slot, dft_table, precision=lax.Precision.HIGH, preferred_element_type=jnp.float32
        )

    transformed = lax.map(column_transform, (slot_grids, blocks_here))
    flat_half = transformed.reshape(SLOTS * BLOCK * 2, CROP)
    row_bases = blocks_here // per_side * BLOCK - GRID // 2
    shifted_rows = row_bases[:, None] + offsets[None, :]
    pixel_rows = (
        jnp.arange(ROWS // lax.axis_size("chan") * lax.axis_size("chan"), dtype=jnp.int32)
        - ROWS // 2
    )
    phase_index = pixel_rows[:, None, None] * shifted_rows[None, :, :] % GRID
    angles = phase_index.astype(jnp.float32) * (TWO_PI / GRID)
    factors = jnp.stack([jnp.cos(angles), -jnp.sin(angles)], axis=3).reshape(
        ROWS // lax.axis_size("chan") * lax.axis_size("chan"), SLOTS * BLOCK * 2
    )
    row_share = lax.psum_scatter(
        jnp.dot(
            factors, flat_half, precision=lax.Precision.HIGH, preferred_element_type=jnp.float32
        )
        / GRID,
        "chan",
        scatter_dimension=0,
        tiled=True,
    )
    return lax.psum_scatter(row_share, "grp", scatter_dimension=1, tiled=True)


def solution(mesh):
    in_specs = (
        P(None, ("grp", "chan"), None),
        P(("grp", "chan"), None, None, None, None),
        P(("grp", "chan"), None, None, None),
        P(("grp", "chan"), None, None, None),
        P(("grp", "chan"), None),
        P(("grp", "chan"), None),
        P(("grp", "chan")),
    )
    out_specs = P("chan", "grp")
    return jax.shard_map(body, mesh=mesh, in_specs=in_specs, out_specs=out_specs, check_vma=False)
```

profile of v0, /device:TPU:1, one launch (start us, length us, event | category | flops | bytes accessed | tf_op | source)
XLA Modules:
  0.0 594.4 jit_solution(6085865454375208146)
XLA Ops:
  6.5 11.5 %all-to-all-start = ((bf16[128,1,16,128]{3,2,1,0:T(8,128)(2,1)}), bf16[128,1,16,128]{3,2,1,0:T(8,128)(2,1)S(1)}, u32[]{:S(2)}, u32[]{:S(2)}) async-start(bf16[128,1,16,128]{3,2,1,0:T(8,128)(2,1)} %bitcast.71), calls=%async_computation | async-start | bytes 1048576 | tf_op jit(solution)/shard_map/all_to_all | solution.py:61
  18.8 8.3 %fusion.43 = (f32[256,16,128,1]{2,1,3,0:T(8,128)S(1)}, f32[256,16,128,1]{2,1,3,0:T(8,128)S(1)}) fusion(s32[16,128]{1,0:T(8,128)S(1)} %iota_add_fusion.2, s32[256]{0:T(256)S(1)} %iota_add_fusion.3), kind=kLoop, calls=%fused_computation.59 | loop fusion | flops 7864320 | bytes 4203520 | tf_op jit(solution)/shard_map/cos | solution.py:99
  30.2 5.9 copy.22
  36.0 6.0 %reshape.138 = f32[256,4096]{0,1:T(8,128)} reshape(f32[256,16,128,2]{0,3,2,1:T(2,128)} %copy.22) | data formatting | bytes 8388608 | tf_op jit(solution)/shard_map/reshape | solution.py:99
  42.1 7.5 %gather_fusion = bf16[136,128,128]{2,1,0:T(8,128)(2,1)} fusion(bf16[16,128,128]{2,1,0:T(8,128)(2,1)S(1)} %bitcast.62, s32[1024]{0:T(1024)S(1)} %pad_clamp_fusion.1), kind=kCustom, calls=%fused_computation | custom fusion | bytes 8913440 | tf_op jit(solution)/shard_map/gather | solution.py:43
  49.7 7.5 %gather_fusion.4 = bf16[136,128,128]{2,1,0:T(8,128)(2,1)} fusion(bf16[16,128,128]{2,1,0:T(8,128)(2,1)S(1)} %bitcast.68, s32[1024]{0:T(1024)S(1)} %pad_clamp_fusion), kind=kCustom, calls=%fused_computation.4 | custom fusion | bytes 8913440 | tf_op jit(solution)/shard_map/gather | solution.py:40
  57.5 7.6 %gather_fusion.1 = bf16[136,128,128]{2,1,0:T(8,128)(2,1)} fusion(bf16[16,128,128]{2,1,0:T(8,128)(2,1)S(1)} %bitcast.64, s32[1024]{0:T(1024)S(1)} %pad_clamp_fusion), kind=kCustom, calls=%fused_computation.1 | custom fusion | bytes 8913440 | tf_op jit(solution)/shard_map/gather | solution.py:30
  65.0 7.7 %gather_fusion.2 = bf16[136,128,128]{2,1,0:T(8,128)(2,1)} fusion(bf16[16,128,128]{2,1,0:T(8,128)(2,1)S(1)} %bitcast.65, s32[1024]{0:T(1024)S(1)} %pad_clamp_fusion.1), kind=kCustom, calls=%fused_computation.2 | custom fusion | bytes 8913440 | tf_op jit(solution)/shard_map/gather | solution.py:32
  73.0 7.5 %gather_fusion.3 = bf16[136,128,128]{2,1,0:T(8,128)(2,1)} fusion(bf16[16,128,128]{2,1,0:T(8,128)(2,1)S(1)} %pad_maximum_fusion.1, s32[1024]{0:T(1024)S(1)} %pad_clamp_fusion.1), kind=kCustom, calls=%fused_computation.3 | custom fusion | bytes 8913440 | tf_op jit(solution)/shard_map/gather | solution.py:35
  80.5 10.4 %convolution_bitcast_fusion.1 = f32[136,1,128,128]{3,2,0,1:T(8,128)} fusion(bf16[136,128,128]{2,1,0:T(8,128)(2,1)} %gather_fusion.1, bf16[136,128,128]{2,1,0:T(8,128)(2,1)} %gather_fusion.3), kind=kOutput, calls=%fused_computation.50 | convolution fusion | flops 570425344 | bytes 17825792 | tf_op jit(solution)/shard_map/kat,kbt->kab/dot_general | solution.py:34
  91.0 8.8 %convolution_bitcast_fusion.2 = f32[136,1,128,128]{3,2,0,1:T(8,128)} fusion(bf16[136,128,128]{2,1,0:T(8,128)(2,1)S(1)} %bitcast.67, bf16[136,128,128]{2,1,0:T(8,128)(2,1)} %gather_fusion.2), kind=kOutput, calls=%fused_computation.51 | convolution fusion | flops 570425344 | bytes 17825792 | tf_op jit(solution)/shard_map/kat,kbt->kab/dot_general | solution.py:31
  99.8 20.4 %fusion.30 = f32[136,128,2,128]{1,3,2,0:T(8,128)} fusion(bf16[136,128,128]{2,1,0:T(8,128)(2,1)} %gather_fusion.4, bf16[136,128,128]{2,1,0:T(8,128)(2,1)} %gather_fusion, f32[136,1,128,128]{3,2,0,1:T(8,128)} %convolution_bitcast_fusion.1, f32[136,1,128,128]{3,2,0,1:T(8,128)} %convolution_bitcast_fusion.2, bf16[1,136,2,128,128]{4,3,2,1,0:T(8,128)(2,1)} %param.17), kind=kOutput, calls=%fused_computation.43 | convolution fusion | flops 2308440064 | bytes 53477376 | tf_op jit(solution)/shard_map/kcub,kvb->kucv/dot_general | solution.py:42
  120.2 26.4 %copy.26 = f32[136,128,2,128]{3,2,1,0:T(2,128)} copy(f32[136,128,2,128]{1,3,2,0:T(8,128)} %fusion.30) | data formatting | bytes 35651584 | tf_op jit(solution)/shard_map/kcub,kvb->kucv/transpose | solution.py:42
  146.6 23.0 %reshape.140 = f32[136,32768]{1,0:T(8,128)} reshape(f32[136,128,2,128]{3,2,1,0:T(2,128)} %copy.26) | data formatting | bytes 35651584 | tf_op jit(solution)/shard_map/reshape | solution.py:51
  169.6 11.8 %convolution_convert_fusion = bf16[16,32768]{1,0:T(8,128)(2,1)S(1)} fusion(f32[136,32768]{1,0:T(8,128)} %reshape.140, f32[136]{0:T(256)S(1)} %compare_convert_fusion, s32[136]{0:T(256)S(1)} %bitcast.73), kind=kOutput, calls=%fused_computation.34 | convolution fusion | flops 856166656 | bytes 18875456 | tf_op jit(solution)/shard_map/dot_general | solution.py:49
  181.6 145.3 %while.14 = (s32[]{:T(128)}, f32[16,128,4096]{2,1,0:T(8,128)}, bf16[16,128,256]{2,1,0:T(8,128)(2,1)S(1)}, s32[16]{0:T(128)S(1)}, s32[]{:T(128)}, /*index=5*/s32[]{:T(128)}, s32[]{:T(128)}, s32[]{:T(128)}, s32[]{:T(128)}) while((s32[]{:T(128)}, f32[16,128,4096]{2,1,0:T(8,128)}, bf16[16,128,256]{2,1,0:T(8,128)(2,1)S(1)}, ...), condition=%wide.region_1.2_spmd.clone, body=%wide.region_0.1_spmd.clone.sunk | while | flops 812386560 | bytes 8472806 | solution.py:89
  184.2 4.2 fusion.67
  193.3 4.2 fusion.67
  202.3 4.2 fusion.67
  211.4 4.2 fusion.67
  326.9 35.7 %reshape.142 = f32[4096,2048]{1,0:T(8,128)} reshape(f32[16,128,4096]{2,1,0:T(8,128)} %get-tuple-element.109) | data formatting | bytes 67108864 | tf_op jit(solution)/shard_map/reshape | solution.py:90
  362.7 19.5 %convolution_multiply_fusion = f32[256,2048]{1,0:T(8,128)} fusion(f32[256,4096]{0,1:T(8,128)} %reshape.138, f32[4096,2048]{1,0:T(8,128)} %reshape.142), kind=kOutput, calls=%fused_computation.54 | convolution fusion | flops 12885426176 | bytes 39845888 | tf_op jit(solution)/shard_map/dot_general | solution.py:103
  382.2 165.9 %reduce-scatter.3.cloned.1.call-done = f32[8,2048]{1,0:T(8,128)} async-done(((f32[256,2048]{1,0:T(8,128)}), f32[8,2048]{1,0:T(8,128)}) %reduce-scatter.3.cloned.1.call-update) | async-done | bytes 65552 | tf_op jit(solution)/shard_map/reduce_scatter | solution.py:102
  548.1 39.2 %reduce-scatter.5.cloned.1.call-done = f32[8,512]{1,0:T(8,128)} async-done(((f32[8,2048]{1,0:T(8,128)}), f32[8,512]{1,0:T(8,128)}) %reduce-scatter.5.cloned.1.call-update) | async-done | bytes 16400 | tf_op jit(solution)/shard_map/reduce_scatter | solution.py:111
  (111 shorter events, 102.3 us)
Async XLA Ops:
  6.5 35.6 %copy-start = (bf16[1,16,128,128]{3,2,1,0:T(8,128)(2,1)S(1)}, bf16[1,16,128,128]{3,2,1,0:T(8,128)(2,1)}, u32[]{:S(2)}) copy-start(bf16[1,16,128,128]{3,2,1,0:T(8,128)(2,1)} %param.19) | copy-start | bytes 1572868
  6.5 50.7 %all-to-all-start = ((bf16[128,1,16,128]{3,2,1,0:T(8,128)(2,1)}), bf16[128,1,16,128]{3,2,1,0:T(8,128)(2,1)S(1)}, u32[]{:S(2)}, u32[]{:S(2)}) async-start(bf16[128,1,16,128]{3,2,1,0:T(8,128)(2,1)} %bitcast.71), calls=%async_computation | async-start | bytes 1048576 | tf_op jit(solution)/shard_map/all_to_all | solution.py:61
  18.0 530.1 %reduce-scatter.3.cloned.1.call-start = ((), (), s32[]{:S(2)}) async-start(), calls=%async_computation.3 | async-start | bytes 2162688 | tf_op jit(solution)/shard_map/reduce_scatter | solution.py:102
  36.0 6.0 %copy-start.5 = (s32[136]{0:T(256)S(1)}, s32[136]{0:T(256)}, u32[]{:S(2)}) copy-start(s32[136]{0:T(256)} %constant.147) | copy-start | bytes 1636
  42.1 7.5 %copy-start.4 = (s32[136]{0:T(256)S(1)}, s32[136]{0:T(256)}, u32[]{:S(2)}) copy-start(s32[136]{0:T(256)} %constant.148) | copy-start | bytes 1636
  42.1 7.5 %copy-start.2 = (bf16[1,16,128,128]{3,2,1,0:T(8,128)(2,1)S(1)}, bf16[1,16,128,128]{3,2,1,0:T(8,128)(2,1)}, u32[]{:S(2)}) copy-start(bf16[1,16,128,128]{3,2,1,0:T(8,128)(2,1)} %param.18) | copy-start | bytes 1572868
  49.7 7.6 %copy-start.3 = (s32[1,136]{1,0:T(1,128)S(1)}, s32[1,136]{1,0:T(1,128)}, u32[]{:S(2)}) copy-start(s32[1,136]{1,0:T(1,128)} %param.20) | copy-start | bytes 1636
  73.0 17.9 %slice-start = ((s8[4456448]{0:T(1024)(128)(4,1)}), s8[262144]{0:T(1024)(128)(4,1)S(1)}, s32[]{:S(2)}) async-start(s8[4456448]{0:T(1024)(128)(4,1)} %bitcast.66), calls=%async_computation.5 | async-start | bytes 524288
  80.5 10.4 %slice-start.1 = ((s8[4456448]{0:T(1024)(128)(4,1)}), s8[4194304]{0:T(1024)(128)(4,1)S(1)}, s32[]{:S(2)}) async-start(s8[4456448]{0:T(1024)(128)(4,1)} %bitcast.66), calls=%async_computation.6 | async-start | bytes 8388608
  169.6 12.0 %copy-start.6 = (s32[1,16]{1,0:T(1,128)S(1)}, s32[1,16]{1,0:T(1,128)}, u32[]{:S(2)}) copy-start(s32[1,16]{1,0:T(1,128)} %param.21) | copy-start | bytes 196
  362.7 224.7 %copy-start.1 = (bf16[1,16,128,128]{3,2,1,0:T(8,128)(2,1)S(1)}, bf16[1,16,128,128]{3,2,1,0:T(8,128)(2,1)}, u32[]{:S(2)}) copy-start(bf16[1,16,128,128]{3,2,1,0:T(8,128)(2,1)} %param.19) | copy-start | bytes 1572868
  382.2 205.1 %reduce-scatter.5.cloned.1.call-start = ((), (), s32[]{:S(2)}) async-start(), calls=%async_computation.4 | async-start | bytes 81920 | tf_op jit(solution)/shard_map/reduce_scatter | solution.py:111
Sparse Core Ops, SparseCore 0:
  382.3 165.7 reduce-scatter.2
  550.5 36.8 reduce-scatter.4
where the time goes:
time: 604 us; the launch traced here: 594 us
  waiting for transfers between devices  205 us (34%)
  local copies, waits for them, and re-layouts  145 us (24%)
  matrix products  109 us (18%)
  other arithmetic  78.7 us (13%)
  loops' own time  30.5 us (5%)
  between operations  14.5 us (2%)
  starting transfers between devices  11.6 us (2%)
    reduce_scatter x1, waiting for transfers between devices, body(): lax.psum_scatter(jnp.dot(factors, flat_half, precision=lax.Precision.HIGH...  166 us
    sin x16, other arithmetic, column_transform(): sine_part = jnp.sin(angles)  66.6 us
    reduce_scatter x1, waiting for transfers between devices, body(): return lax.psum_scatter(row_share, 'grp', scatter_dimension=1, tiled=True)  39.2 us
    dot_general x16, matrix products, column_transform(): jnp.dot(grid_slot, dft_table, precision=lax.Precision.HIGH, preferred_ele...  37.9 us
    reshape x1, local copies, waits for them, and re-layouts, body(): flat_half = transformed.reshape(SLOTS * BLOCK * 2, CROP)  35.7 us
    another operation x1, loops' own time, body(): transformed = lax.map(column_transform, (slot_grids, blocks_here))  30.5 us
    transpose x1, local copies, waits for them, and re-layouts, grid_channel(): jnp.einsum('kcub,kvb->kucv', half_grid, kernel_v_one[col_tiles], preferre...  26.4 us
    reshape x1, local copies, waits for them, and re-layouts, grid_channel(): tile_grid.reshape(PAIRS, BLOCK * 2 * BLOCK)  23 us
  transfers between devices with their start and end apart: 3, of which 2 were waited for; matrix products, arithmetic and copies ran while one was open for 6% of the time, Pallas kernels for 0%

commit v1 on v0

v1 whole, which is shorter than its diff:
```python
import math

import jax
import jax.numpy as jnp
import numpy as np
from jax import lax
from jax.experimental import pallas as pl
from jax.experimental.pallas import tpu as pltpu
from jax.sharding import PartitionSpec as P

ANTENNAS = 2048
SAMPLES = 64
TILE = 128
BLOCK = 128
GRID = 4096
CROP = 2048
SLOTS = 16
ROWS = 256
TILES = 16
PAIRS = 136
PHASES = 32

TWO_PI = 2.0 * math.pi


def _grid_kernel(ptab, qtab, slot_ref, count_ref, v_ref, s_ref, model_ref, ku_ref, kv_ref, out_ref, acc_ref):
    acc_ref[...] = jnp.zeros_like(acc_ref)
    count = count_ref[0]
    nt = (((1,), (1,)), ((), ()))

    def body(k, carry):
        p = ptab[k]
        q = qtab[k]
        slot = slot_ref[k]
        p0 = pl.multiple_of(p * TILE, TILE)
        q0 = pl.multiple_of(q * TILE, TILE)
        vp = v_ref[pl.ds(p0, TILE), :]
        vq = v_ref[pl.ds(q0, TILE), :]
        sq = s_ref[pl.ds(q0, TILE), :]
        rhs = jnp.concatenate([vq, sq], axis=0)
        gram = lax.dot_general(vp, rhs, nt, preferred_element_type=jnp.float32)
        model = jnp.concatenate([model_ref[k, 0], model_ref[k, 1]], axis=1).astype(jnp.float32)
        residual = (gram * (1.0 / SAMPLES) - model).astype(jnp.bfloat16)
        half = jnp.dot(ku_ref[p], residual, preferred_element_type=jnp.float32).astype(jnp.bfloat16)
        half_rows = jnp.concatenate([half[:, :TILE], half[:, TILE:]], axis=0)
        tile = lax.dot_general(half_rows, kv_ref[q], nt, preferred_element_type=jnp.float32)
        live = (slot < count) & (slot >= 0)
        slot_c = jnp.clip(slot, 0, SLOTS - 1)

        @pl.when(live)
        def _():
            acc_ref[slot_c] += tile

        return carry

    lax.fori_loop(0, PAIRS, body, 0)
    out_ref[...] = acc_ref[...].astype(out_ref.dtype)


def grid_slots(antenna_volts, model_one, kernel_u_one, kernel_v_one, slots_one, count_one):
    row_tiles, col_tiles = np.triu_indices(TILES)
    ptab = jnp.asarray(row_tiles, jnp.int32)
    qtab = jnp.asarray(col_tiles, jnp.int32)
    swapped = jnp.concatenate([-antenna_volts[:, SAMPLES:], antenna_volts[:, :SAMPLES]], axis=1)
    smem = pl.BlockSpec(memory_space=pltpu.SMEM)
    vmem = pl.BlockSpec(memory_space=pltpu.VMEM)
    flops = PAIRS * 3 * 2 * (2 * TILE) * TILE * TILE
    return pl.pallas_call(
        _grid_kernel,
        out_shape=jax.ShapeDtypeStruct((SLOTS, 2 * BLOCK, BLOCK), jnp.bfloat16),
        in_specs=[smem, smem, smem, smem, vmem, vmem, vmem, vmem, vmem],
        out_specs=vmem,
        scratch_shapes=[pltpu.VMEM((SLOTS, 2 * BLOCK, BLOCK), jnp.float32)],
        compiler_params=pltpu.CompilerParams(vmem_limit_bytes=48 * 1024 * 1024),
        cost_estimate=pl.CostEstimate(flops=flops, transcendentals=0, bytes_accessed=11 * 1024 * 1024),
    )(ptab, qtab, slots_one, count_one, antenna_volts, swapped, model_one, kernel_u_one, kernel_v_one)


def _cos_sin(index, period):
    angles = index.astype(jnp.float32) * (TWO_PI / period)
    return jnp.cos(angles), jnp.sin(angles)


def channel_image(slot_grids, blocks_here):
    per_side = GRID // BLOCK
    grids = slot_grids.reshape(SLOTS, 2, BLOCK, BLOCK).astype(jnp.float32)
    block_rows = blocks_here // per_side
    block_cols = blocks_here % per_side
    offsets = jnp.arange(BLOCK, dtype=jnp.int32)
    pixel_rows = jnp.arange(ROWS, dtype=jnp.int32) - ROWS // 2
    grid_rows = block_rows[:, None] * BLOCK + offsets[None, :] - GRID // 2
    ar, ai = _cos_sin(jnp.mod(pixel_rows[None, :, None] * grid_rows[:, None, :], GRID), GRID)
    row_op = jnp.stack([jnp.stack([ar, -ai], axis=2), jnp.stack([ai, ar], axis=2)], axis=1)
    rows_done = jnp.einsum(
        "sclku,skuv->sclv", row_op, grids, precision=lax.Precision.HIGH, preferred_element_type=jnp.float32
    )
    phases = jnp.arange(PHASES, dtype=jnp.int32)
    zr, zi = _cos_sin(jnp.mod(phases[:, None] * block_cols[None, :], PHASES), PHASES)
    phase_op = jnp.stack([jnp.stack([zr, -zi], axis=2), jnp.stack([zi, zr], axis=2)], axis=1)
    summed = jnp.einsum(
        "tcsk,sklv->tclv", phase_op, rows_done, precision=lax.Precision.HIGH, preferred_element_type=jnp.float32
    )
    col_groups = jnp.arange(CROP // PHASES, dtype=jnp.int32)
    pixel_cols = col_groups[None, :] * PHASES + phases[:, None] - CROP // 2
    br, bi = _cos_sin(jnp.mod(pixel_cols[:, None, :] * (offsets - GRID // 2)[None, :, None], GRID), GRID)
    col_op = jnp.stack([br, -bi], axis=1)
    return jnp.einsum(
        "tclv,tcvj->tlj", summed, col_op, precision=lax.Precision.HIGH, preferred_element_type=jnp.float32
    ) * (1.0 / GRID)


def body(voltages, model_vis, kernel_u, kernel_v, pair_slot, slot_block, slot_count):
    local_antennas = voltages.shape[1]
    direct = voltages.reshape(voltages.shape[0], 1, local_antennas, 2 * SAMPLES)
    turned = lax.all_to_all(direct, ("grp", "chan"), split_axis=0, concat_axis=1, tiled=True)
    antenna_volts = turned.reshape(ANTENNAS, 2 * SAMPLES)
    slot_grids = grid_slots(
        antenna_volts, model_vis[0], kernel_u[0], kernel_v[0], pair_slot[0], slot_count
    )
    image_t = channel_image(slot_grids, slot_block[0])
    n_chan = lax.axis_size("chan")
    n_grp = lax.axis_size("grp")
    rows_per = ROWS // n_chan
    groups_per = CROP // PHASES // n_grp
    send = image_t.reshape(PHASES, n_chan, rows_per, n_grp, groups_per).transpose(1, 3, 2, 4, 0)
    send = send.reshape(n_chan * n_grp, rows_per, groups_per, PHASES)
    got = lax.all_to_all(send, ("chan", "grp"), split_axis=0, concat_axis=0, tiled=True)
    return got.sum(axis=0).reshape(rows_per, groups_per * PHASES)


def solution(mesh):
    in_specs = (
        P(None, ("grp", "chan"), None),
        P(("grp", "chan"), None, None, None, None),
        P(("grp", "chan"), None, None, None),
        P(("grp", "chan"), None, None, None),
        P(("grp", "chan"), None),
        P(("grp", "chan"), None),
        P(("grp", "chan")),
    )
    out_specs = P("chan", "grp")
    return jax.shard_map(body, mesh=mesh, in_specs=in_specs, out_specs=out_specs, check_vma=False)
```

time: 604 us -> 198 us (0.33); the launches traced: 594 us -> 197 us
  waiting for transfers between devices: 205 us -> 0.01 us
  local copies, waits for them, and re-layouts: 145 us -> 28.9 us
  matrix products: 109 us -> 16.5 us
  Pallas kernels: 0 us -> 68.3 us
  other arithmetic: 78.7 us -> 31.7 us
  blocking collectives: 0 us -> 39.5 us
  loops' own time: 30.5 us -> 0 us
  between operations: 14.5 us -> 0.82 us
    reduce_scatter x2 -> x0, waiting for transfers between devices: 205 us -> none  [the longest x1 166 us: body(): lax.psum_scatter(jnp.dot(factors, flat_half, precision=lax.Precision.HIGH...]
    dot_general x21 -> x3, matrix products: 109 us -> 16.5 us  [the longest x1 8.37 us: channel_image(): jnp.einsum('tclv,tcvj->tlj', summed, col_op, precision=lax.Precision.HIGH...]
    pallas_call x0 -> x1, Pallas kernels: none -> 68.3 us  [grid_slots(): pl.pallas_call(_grid_kernel, out_shape=jax.ShapeDtypeStruct((SLOTS, 2 * B...]
    sin x16 -> x0, other arithmetic: 66.6 us -> none  [column_transform(): sine_part = jnp.sin(angles)]
    reshape x3 -> x1, local copies, waits for them, and re-layouts: 64.7 us -> 0.69 us  [body(): return got.sum(axis=0).reshape(rows_per, groups_per * PHASES)]
    all_to_all x0 -> x1, blocking collectives: none -> 39.5 us  [body(): lax.all_to_all(send, ('chan', 'grp'), split_axis=0, concat_axis=0, tiled=...]
    gather x5 -> x0, local copies, waits for them, and re-layouts: 37.7 us -> none  [the longest x1 7.66 us: grid_channel(): antenna_tiles[col_tiles]]
    another operation x1 -> x0, loops' own time: 30.5 us -> none  [body(): transformed = lax.map(column_transform, (slot_grids, blocks_here))]
  transfers between devices with their start and end apart: 3 -> 1, of which waited for: 2 -> 0; matrix products, arithmetic and copies ran while one was open for 6% -> 10% of each run, Pallas kernels for 0% -> 0%
where the time goes in v1:
time: 198 us; the launch traced here: 197 us
  Pallas kernels  68.3 us (34%)
  blocking collectives  39.5 us (20%)
  other arithmetic  31.7 us (16%)
  local copies, waits for them, and re-layouts  28.9 us (15%)
  matrix products  16.5 us (8%)
  starting transfers between devices  11.5 us (6%)
    pallas_call x1, Pallas kernels, grid_slots(): pl.pallas_call(_grid_kernel, out_shape=jax.ShapeDtypeStruct((SLOTS, 2 * B...  68.3 us
    all_to_all x1, blocking collectives, body(): lax.all_to_all(send, ('chan', 'grp'), split_axis=0, concat_axis=0, tiled=...  39.5 us
    unnamed x18, local copies, waits for them, and re-layouts  12.3 us
    all_to_all x1, starting transfers between devices, body(): lax.all_to_all(direct, ('grp', 'chan'), split_axis=0, concat_axis=1, tile...  11.5 us
    dot_general x1, matrix products, channel_image(): jnp.einsum('tclv,tcvj->tlj', summed, col_op, precision=lax.Precision.HIGH...  8.37 us
    neg x1, other arithmetic, channel_image(): -ai  8.37 us
    transpose x1, local copies, waits for them, and re-layouts, body(): image_t.reshape(PHASES, n_chan, rows_per, n_grp, groups_per)  7.92 us
    mul x1, local copies, waits for them, and re-layouts, channel_image(): jnp.einsum('tclv,tcvj->tlj', summed, col_op, precision=lax.Precision.HIGH...  7.53 us
  transfers between devices with their start and end apart: 1, of which 0 were waited for; matrix products, arithmetic and copies ran while one was open for 10% of the time, Pallas kernels for 0%

profile of v1, /device:TPU:1, one launch (start us, length us, event | category | flops | bytes accessed | tf_op | source)
XLA Modules:
  0.0 197.3 jit_solution(11699813389110246985)
XLA Ops:
  0.0 11.5 %all-to-all-start = ((bf16[128,1,16,128]{3,2,1,0:T(8,128)(2,1)}), bf16[128,1,16,128]{3,2,1,0:T(8,128)(2,1)S(1)}, u32[]{:S(2)}, u32[]{:S(2)}) async-start(bf16[128,1,16,128]{3,2,1,0:T(8,128)(2,1)} %bitcast.65), calls=%async_computation | async-start | bytes 1048576 | tf_op jit(solution)/shard_map/all_to_all | solution.py:115
  11.5 0.7 fusion.45
  12.2 0.7 fusion.43
  13.6 0.1 fusion.42
  13.7 8.4 %fusion.30 = (f32[16,256,1,128]{3,1,2,0:T(8,128)S(1)}, f32[16,256,1,128]{3,1,2,0:T(8,128)S(1)}, f32[16,256,1,128]{3,1,2,0:T(8,128)S(1)}) fusion(s32[16,128]{1,0:T(8,128)S(1)} %add_add_fusion.1, s32[256]{0:T(256)S(1)} %iota_add_fusion), kind=kLoop, calls=%fused_computation.36 | loop fusion | flops 7864320 | bytes 6300672 | tf_op jit(solution)/shard_map/neg | solution.py:93
  22.1 5.7 %fusion.31 = (f32[32,1,128,64]{2,3,1,0:T(8,128)S(1)}, f32[32,1,128,64]{2,3,1,0:T(8,128)}) fusion(s32[128]{0:T(128)S(1)} %iota_add_fusion.1, s32[32,64]{1,0:T(8,128)S(1)} %add_add_fusion), kind=kLoop, calls=%fused_computation.39 | loop fusion | flops 3932160 | bytes 2105856 | tf_op jit(solution)/shard_map/cos | solution.py:81
  27.8 4.2 %maximum_bitcast_fusion = (f32[16,1,256,2,128]{4,2,3,1,0:T(8,128)}, f32[16,1,256,2,128]{4,2,3,1,0:T(8,128)}) fusion(f32[16,256,1,128]{3,1,2,0:T(8,128)S(1)} %get-tuple-element.11, f32[16,256,1,128]{3,1,2,0:T(8,128)S(1)} %get-tuple-element.13, f32[16,256,1,128]{3,1,2,0:T(8,128)S(1)} %get-tuple-element.12), kind=kLoop, calls=%fused_computation.6 | loop fusion | flops 2097152 | bytes 14680064 | tf_op jit(solution)/shard_map/stack | solution.py:93
  32.0 0.2 slice_negate_fusion
  32.3 0.3 pad_maximum_fusion.s_ref
  32.6 0.5 copy-done
  33.1 0.2 copy-done.1
  33.2 68.3 %shard_map.91 = bf16[16,256,128]{2,1,0:T(8,128)(2,1)S(1)} custom-call(s32[136]{0:T(256)S(1)} %copy-done.3, s32[136]{0:T(256)S(1)} %copy-done.4, s32[136]{0:T(256)S(1)} %bitcast.62, s32[1]{0:T(128)S(6)} %copy.32.count_ref, bf16[2048,128]{1,0:T(8,128)(2,1)S(1)} %bitcast.58, bf16[2048,128]{1,0:T(8,128)(2,1)S(1)} %pad_maximum_fusion.s_ref, ...), custom_call_target="tpu_custom_call" | custom-call | flops 3422552064 | bytes 11534336 | tf_op jit(solution)/shard_map/pallas_call | solution.py:68
  101.5 2.3 %fusion.12 = f32[16,2,256,128]{3,2,1,0:T(8,128)S(1)} fusion(bf16[16,2,128,128,1]{3,2,1,4,0:T(8,128)(2,1)S(1)} %bitcast.59, f32[16,1,256,2,128]{4,2,3,1,0:T(8,128)S(1)} %copy-done.6, f32[16,1,256,2,128]{4,2,3,1,0:T(8,128)S(1)} %copy-done.5), kind=kOutput, calls=%fused_computation.17 | convolution fusion | flops 1612709888 | bytes 13631488 | tf_op jit(solution)/shard_map/sclku,skuv->sclv/dot_general | solution.py:94
  103.9 5.8 %fusion.9 = f32[32,2,256,128]{3,0,2,1:T(8,128)S(1)} fusion(f32[16,2,256,128]{3,2,1,0:T(8,128)S(1)} %fusion.12, f32[32,1,16,2]{0,2,3,1:T(8,128)S(1)} %get-tuple-element.15, f32[32,1,16,2]{0,2,3,1:T(8,128)S(1)} %get-tuple-element.14), kind=kOutput, calls=%fused_computation.14 | convolution fusion | flops 402655232 | bytes 12591104 | tf_op jit(solution)/shard_map/tcsk,sklv->tclv/dot_general | solution.py:100
  109.7 8.4 %bitcast_multiply_fusion = f32[32,256,64]{1,2,0:T(8,128)S(1)} fusion(f32[32,1,128,64]{2,3,1,0:T(8,128)S(1)} %copy-done.7, f32[32,1,128,64]{2,3,1,0:T(8,128)S(1)} %get-tuple-element.9, f32[32,2,256,128]{3,0,2,1:T(8,128)S(1)} %fusion.9), kind=kOutput, calls=%fused_computation.24 | convolution fusion | flops 806354944 | bytes 12582912 | tf_op jit(solution)/shard_map/tclv,tcvj->tlj/dot_general | solution.py:107
  118.1 7.5 %copy.15 = f32[32,256,64]{0,2,1:T(8,128)} copy(f32[32,256,64]{1,2,0:T(8,128)S(1)} %bitcast_multiply_fusion) | data formatting | bytes 4194304 | tf_op jit(solution)/shard_map/mul | solution.py:107
  125.6 7.9 %copy.16 = f32[32,4,8,16,32]{4,3,2,1,0:T(8,128)} copy(f32[32,4,8,16,32]{4,3,1,2,0:T(8,128)} %bitcast.63) | data formatting | bytes 4194304 | tf_op jit(solution)/shard_map/transpose | solution.py:125
  133.5 6.8 %reshape.365 = f32[128,1,4096]{2,1,0:T(1,128)S(1)} reshape(f32[128,8,16,32]{3,2,1,0:T(8,128)} %bitcast.64) | data formatting | bytes 4194304
  140.4 39.5 %all_to_all.14 = f32[128,1,4096]{2,1,0:T(1,128)} all-to-all(f32[128,1,4096]{2,1,0:T(1,128)S(1)} %reshape.365), channel_id=1, replica_groups=mesh['grp'=4,'chan'=32] {'chan','grp'}, dimensions={0} | all-to-all | bytes 4194304 | tf_op jit(solution)/shard_map/all_to_all | solution.py:127
  179.9 0.5 broadcast.499
  180.4 7.3 %reduce = f32[128,4096]{1,0:T(8,128)S(1)} reduce(f32[128,1,4096]{2,1,0:T(1,128)} %all_to_all.14, f32[]{:T(128)} %broadcast.499), dimensions={1}, to_apply=%all_to_all.5.reduce_sub_computation | reduce | bytes 4194308 | tf_op jit(solution)/shard_map/all_to_all | solution.py:127
  187.7 4.8 %reshape.366 = f32[128,8,16,32]{3,2,1,0:T(8,128)} reshape(f32[128,4096]{1,0:T(8,128)S(1)} %reduce) | data formatting | bytes 4194304
  192.5 4.1 %reduce_sum.9 = f32[8,16,32]{2,1,0:T(8,128)S(1)} reduce(f32[128,8,16,32]{3,2,1,0:T(8,128)} %reshape.366, f32[]{:T(128)} %constant.84.clone.1), dimensions={0}, to_apply=%region_0.1 | reduce | flops 520192 | bytes 2113540 | tf_op jit(solution)/shard_map/reduce_sum | solution.py:128
  196.6 0.7 reshape.358
  (21 shorter events, 0.1 us)
Async XLA Ops:
  0.0 32.0 %all-to-all-start = ((bf16[128,1,16,128]{3,2,1,0:T(8,128)(2,1)}), bf16[128,1,16,128]{3,2,1,0:T(8,128)(2,1)S(1)}, u32[]{:S(2)}, u32[]{:S(2)}) async-start(bf16[128,1,16,128]{3,2,1,0:T(8,128)(2,1)} %bitcast.65), calls=%async_computation | async-start | bytes 1048576 | tf_op jit(solution)/shard_map/all_to_all | solution.py:115
  32.0 1.0 copy-start
  32.0 1.2 copy-start.1
  32.0 1.2 copy-start.2
  32.0 1.2 copy-start.3
  32.0 1.2 copy-start.4
  33.2 68.3 %copy-start.5 = (f32[16,1,256,2,128]{4,2,3,1,0:T(8,128)S(1)}, f32[16,1,256,2,128]{4,2,3,1,0:T(8,128)}, u32[]{:S(2)}) copy-start(f32[16,1,256,2,128]{4,2,3,1,0:T(8,128)} %get-tuple-element.5) | copy-start | bytes 12582916
  33.2 68.3 %copy-start.6 = (f32[16,1,256,2,128]{4,2,3,1,0:T(8,128)S(1)}, f32[16,1,256,2,128]{4,2,3,1,0:T(8,128)}, u32[]{:S(2)}) copy-start(f32[16,1,256,2,128]{4,2,3,1,0:T(8,128)} %get-tuple-element.6) | copy-start | bytes 12582916
  103.9 5.8 %copy-start.7 = (f32[32,1,128,64]{2,3,1,0:T(8,128)S(1)}, f32[32,1,128,64]{2,3,1,0:T(8,128)}, u32[]{:S(2)}) copy-start(f32[32,1,128,64]{2,3,1,0:T(8,128)} %get-tuple-element.10) | copy-start | bytes 3145732

commit v2 on v1

--- a/solution.py
+++ b/solution.py
@@ -23,27 +23,20 @@
 TWO_PI = 2.0 * math.pi
 
 
-def _grid_kernel(ptab, qtab, slot_ref, count_ref, v_ref, s_ref, model_ref, ku_ref, kv_ref, out_ref, acc_ref):
+def _grid_kernel(ptab, qtab, slot_ref, count_ref, v_ref, w_ref, model_ref, ku_ref, kvt_ref, out_ref, acc_ref):
     acc_ref[...] = jnp.zeros_like(acc_ref)
     count = count_ref[0]
-    nt = (((1,), (1,)), ((), ()))
 
     def body(k, carry):
         p = ptab[k]
         q = qtab[k]
         slot = slot_ref[k]
-        p0 = pl.multiple_of(p * TILE, TILE)
-        q0 = pl.multiple_of(q * TILE, TILE)
-        vp = v_ref[pl.ds(p0, TILE), :]
-        vq = v_ref[pl.ds(q0, TILE), :]
-        sq = s_ref[pl.ds(q0, TILE), :]
-        rhs = jnp.concatenate([vq, sq], axis=0)
-        gram = lax.dot_general(vp, rhs, nt, preferred_element_type=jnp.float32)
+        gram = jnp.dot(v_ref[p], w_ref[q], preferred_element_type=jnp.float32)
         model = jnp.concatenate([model_ref[k, 0], model_ref[k, 1]], axis=1).astype(jnp.float32)
         residual = (gram * (1.0 / SAMPLES) - model).astype(jnp.bfloat16)
         half = jnp.dot(ku_ref[p], residual, preferred_element_type=jnp.float32).astype(jnp.bfloat16)
         half_rows = jnp.concatenate([half[:, :TILE], half[:, TILE:]], axis=0)
-        tile = lax.dot_general(half_rows, kv_ref[q], nt, preferred_element_type=jnp.float32)
+        tile = jnp.dot(half_rows, kvt_ref[q], preferred_element_type=jnp.float32)
         live = (slot < count) & (slot >= 0)
         slot_c = jnp.clip(slot, 0, SLOTS - 1)
 
@@ -53,7 +46,7 @@
 
         return carry
 
-    lax.fori_loop(0, PAIRS, body, 0)
+    lax.fori_loop(0, PAIRS, body, 0, unroll=4)
     out_ref[...] = acc_ref[...].astype(out_ref.dtype)
 
 
@@ -62,6 +55,11 @@
     ptab = jnp.asarray(row_tiles, jnp.int32)
     qtab = jnp.asarray(col_tiles, jnp.int32)
     swapped = jnp.concatenate([-antenna_volts[:, SAMPLES:], antenna_volts[:, :SAMPLES]], axis=1)
+    tiles = antenna_volts.reshape(TILES, TILE, 2 * SAMPLES)
+    turned = jnp.concatenate(
+        [tiles.transpose(0, 2, 1), swapped.reshape(TILES, TILE, 2 * SAMPLES).transpose(0, 2, 1)], axis=2
+    )
+    kv_turned = kernel_v_one.transpose(0, 2, 1)
     smem = pl.BlockSpec(memory_space=pltpu.SMEM)
     vmem = pl.BlockSpec(memory_space=pltpu.VMEM)
     flops = PAIRS * 3 * 2 * (2 * TILE) * TILE * TILE
@@ -73,7 +71,7 @@
         scratch_shapes=[pltpu.VMEM((SLOTS, 2 * BLOCK, BLOCK), jnp.float32)],
         compiler_params=pltpu.CompilerParams(vmem_limit_bytes=48 * 1024 * 1024),
         cost_estimate=pl.CostEstimate(flops=flops, transcendentals=0, bytes_accessed=11 * 1024 * 1024),
-    )(ptab, qtab, slots_one, count_one, antenna_volts, swapped, model_one, kernel_u_one, kernel_v_one)
+    )(ptab, qtab, slots_one, count_one, tiles, turned, model_one, kernel_u_one, kv_turned)
 
 
 def _cos_sin(index, period):
@@ -122,10 +120,11 @@
     n_grp = lax.axis_size("grp")
     rows_per = ROWS // n_chan
     groups_per = CROP // PHASES // n_grp
-    send = image_t.reshape(PHASES, n_chan, rows_per, n_grp, groups_per).transpose(1, 3, 2, 4, 0)
-    send = send.reshape(n_chan * n_grp, rows_per, groups_per, PHASES)
+    send = image_t.reshape(PHASES, n_chan, rows_per, n_grp, groups_per).transpose(1, 3, 0, 2, 4)
+    send = send.reshape(n_chan * n_grp, PHASES * rows_per * groups_per)
     got = lax.all_to_all(send, ("chan", "grp"), split_axis=0, concat_axis=0, tiled=True)
-    return got.sum(axis=0).reshape(rows_per, groups_per * PHASES)
+    summed = got.sum(axis=0).reshape(PHASES, rows_per, groups_per)
+    return summed.transpose(1, 2, 0).reshape(rows_per, groups_per * PHASES)
 
 
 def solution(mesh):

time: 198 us -> 192 us (0.970)
  other arithmetic: 31.7 us -> 23.4 us
  local copies, waits for them, and re-layouts: 28.9 us -> 34.3 us
  Pallas kernels: 68.3 us -> 65.4 us
    all_to_all x1, local copies, waits for them, and re-layouts: 0.51 us -> 11.4 us  [body(): lax.all_to_all(send, ('chan', 'grp'), split_axis=0, concat_axis=0, tiled=...]
    unnamed x18 -> x17, local copies, waits for them, and re-layouts: 12.3 us -> 1.61 us
    all_to_all x1 -> x0, other arithmetic: 7.31 us -> none  [body(): lax.all_to_all(send, ('chan', 'grp'), split_axis=0, concat_axis=0, tiled=...]
    transpose x1, local copies, waits for them, and re-layouts: 7.92 us -> 12.3 us  [body(): image_t.reshape(PHASES, n_chan, rows_per, n_grp, groups_per)]
    pallas_call x1, Pallas kernels: 68.3 us -> 65.4 us  [grid_slots(): pl.pallas_call(_grid_kernel, out_shape=jax.ShapeDtypeStruct((SLOTS, 2 * B...]
  transfers between devices with their start and end apart: 1 -> 1, of which waited for: 0 -> 0; matrix products, arithmetic and copies ran while one was open for 10% -> 11% of each run, Pallas kernels for 0% -> 0%
where the time goes in v2:
time: 192 us
  Pallas kernels  65.4 us (34%)
  blocking collectives  39.6 us (21%)
  local copies, waits for them, and re-layouts  34.3 us (18%)
  other arithmetic  23.4 us (12%)
  matrix products  16.5 us (9%)
  starting transfers between devices  11.5 us (6%)
    pallas_call x1, Pallas kernels, grid_slots(): pl.pallas_call(_grid_kernel, out_shape=jax.ShapeDtypeStruct((SLOTS, 2 * B...  65.4 us
    all_to_all x1, blocking collectives, body(): lax.all_to_all(send, ('chan', 'grp'), split_axis=0, concat_axis=0, tiled=...  39.6 us
    transpose x1, local copies, waits for them, and re-layouts, body(): image_t.reshape(PHASES, n_chan, rows_per, n_grp, groups_per)  12.3 us
    all_to_all x1, starting transfers between devices, body(): lax.all_to_all(direct, ('grp', 'chan'), split_axis=0, concat_axis=1, tile...  11.5 us
    all_to_all x1, local copies, waits for them, and re-layouts, body(): lax.all_to_all(send, ('chan', 'grp'), split_axis=0, concat_axis=0, tiled=...  11.4 us
    dot_general x1, matrix products, channel_image(): jnp.einsum('tclv,tcvj->tlj', summed, col_op, precision=lax.Precision.HIGH...  8.37 us
    neg x1, other arithmetic, channel_image(): -ai  8.37 us
    mul x1, local copies, waits for them, and re-layouts, channel_image(): jnp.einsum('tclv,tcvj->tlj', summed, col_op, precision=lax.Precision.HIGH...  7.55 us
  transfers between devices with their start and end apart: 1, of which 0 were waited for; matrix products, arithmetic and copies ran while one was open for 11% of the time, Pallas kernels for 0%

profile of v2, /device:TPU:1, one launch (start us, length us, event | category | flops | bytes accessed | tf_op | source)
XLA Modules:
  0.0 191.6 jit_solution(158512280113950106)
XLA Ops:
  0.0 11.5 %all-to-all-start = ((bf16[128,1,16,128]{3,2,1,0:T(8,128)(2,1)}), bf16[128,1,16,128]{3,2,1,0:T(8,128)(2,1)S(1)}, u32[]{:S(2)}, u32[]{:S(2)}) async-start(bf16[128,1,16,128]{3,2,1,0:T(8,128)(2,1)} %bitcast.77), calls=%async_computation | async-start | bytes 1048576 | tf_op jit(solution)/shard_map/all_to_all | solution.py:113
  11.5 0.7 fusion.45
  12.2 0.7 fusion.43
  13.6 0.1 fusion.42
  13.7 1.3 copy.29
  15.0 8.4 %fusion.30 = (f32[16,256,1,128]{3,1,2,0:T(8,128)S(1)}, f32[16,256,1,128]{3,1,2,0:T(8,128)S(1)}, f32[16,256,1,128]{3,1,2,0:T(8,128)S(1)}) fusion(s32[16,128]{1,0:T(8,128)S(1)} %add_add_fusion.1, s32[256]{0:T(256)S(1)} %iota_add_fusion), kind=kLoop, calls=%fused_computation.37 | loop fusion | flops 7864320 | bytes 6300672 | tf_op jit(solution)/shard_map/neg | solution.py:91
  23.4 5.8 %fusion.31 = (f32[32,1,128,64]{2,3,1,0:T(8,128)}, f32[32,1,128,64]{2,3,1,0:T(8,128)}) fusion(s32[128]{0:T(128)S(1)} %iota_add_fusion.1, s32[32,64]{1,0:T(8,128)S(1)} %add_add_fusion), kind=kLoop, calls=%fused_computation.40 | loop fusion | flops 3932160 | bytes 2105856 | tf_op jit(solution)/shard_map/cos | solution.py:79
  29.2 4.2 %maximum_bitcast_fusion = (f32[16,1,256,2,128]{4,2,3,1,0:T(8,128)}, f32[16,1,256,2,128]{4,2,3,1,0:T(8,128)}) fusion(f32[16,256,1,128]{3,1,2,0:T(8,128)S(1)} %get-tuple-element.11, f32[16,256,1,128]{3,1,2,0:T(8,128)S(1)} %get-tuple-element.13, f32[16,256,1,128]{3,1,2,0:T(8,128)S(1)} %get-tuple-element.12), kind=kLoop, calls=%fused_computation.6 | loop fusion | flops 2097152 | bytes 14680064 | tf_op jit(solution)/shard_map/stack | solution.py:91
  33.5 0.3 copy.27
  33.8 0.2 slice_negate_fusion
  34.0 0.3 pad_maximum_fusion.1
  34.3 0.3 copy.28
  34.6 0.1 pad_maximum_fusion.w_ref
  34.8 0.3 copy-done
  35.1 65.4 %shard_map.91 = bf16[16,256,128]{2,1,0:T(8,128)(2,1)S(1)} custom-call(s32[136]{0:T(256)S(1)} %copy-done.3, s32[136]{0:T(256)S(1)} %copy-done.2, s32[136]{0:T(256)S(1)} %bitcast.71, s32[1]{0:T(128)S(6)} %copy.51.count_ref, bf16[16,128,128]{2,1,0:T(8,128)(2,1)S(1)} %bitcast.67, bf16[16,128,256]{2,1,0:T(8,128)(2,1)S(1)} %pad_maximum_fusion.w_ref, ...), custom_call_target="tpu_custom_call" | custom-call | flops 3422552064 | bytes 11534336 | tf_op jit(solution)/shard_map/pallas_call | solution.py:66
  100.5 2.3 %fusion.12 = f32[16,2,256,128]{3,2,1,0:T(8,128)S(1)} fusion(bf16[16,2,128,128,1]{3,2,1,4,0:T(8,128)(2,1)S(1)} %bitcast.68, f32[16,1,256,2,128]{4,2,3,1,0:T(8,128)S(1)} %copy-done.5, f32[16,1,256,2,128]{4,2,3,1,0:T(8,128)S(1)} %copy-done.4), kind=kOutput, calls=%fused_computation.17 | convolution fusion | flops 1612709888 | bytes 13631488 | tf_op jit(solution)/shard_map/sclku,skuv->sclv/dot_general | solution.py:92
  102.9 5.8 %fusion.9 = f32[32,2,256,128]{3,0,2,1:T(8,128)S(1)} fusion(f32[16,2,256,128]{3,2,1,0:T(8,128)S(1)} %fusion.12, f32[32,1,16,2]{0,2,3,1:T(8,128)S(1)} %get-tuple-element.15, f32[32,1,16,2]{0,2,3,1:T(8,128)S(1)} %get-tuple-element.14), kind=kOutput, calls=%fused_computation.14 | convolution fusion | flops 402655232 | bytes 12591104 | tf_op jit(solution)/shard_map/tcsk,sklv->tclv/dot_general | solution.py:98
  108.7 8.4 %bitcast_multiply_fusion = f32[32,256,64]{1,2,0:T(8,128)S(1)} fusion(f32[32,1,128,64]{2,3,1,0:T(8,128)S(1)} %copy-done.7, f32[32,1,128,64]{2,3,1,0:T(8,128)S(1)} %copy-done.6, f32[32,2,256,128]{3,0,2,1:T(8,128)S(1)} %fusion.9), kind=kOutput, calls=%fused_computation.24 | convolution fusion | flops 806354944 | bytes 12582912 | tf_op jit(solution)/shard_map/tclv,tcvj->tlj/dot_general | solution.py:105
  117.1 7.6 %copy.32 = f32[32,256,64]{0,2,1:T(8,128)} copy(f32[32,256,64]{1,2,0:T(8,128)S(1)} %bitcast_multiply_fusion) | data formatting | bytes 4194304 | tf_op jit(solution)/shard_map/mul | solution.py:105
  124.6 12.3 %copy.33 = f32[32,4,32,8,16]{4,3,2,1,0:T(8,128)} copy(f32[32,4,32,8,16]{2,4,1,3,0:T(8,128)} %bitcast.72) | data formatting | bytes 4194304 | tf_op jit(solution)/shard_map/transpose | solution.py:123
  136.9 11.4 %all_to_all.16 = f32[128,1,4096]{2,1,0:T(1,128)S(1)} reshape(f32[32,4,32,8,16]{4,3,2,1,0:T(8,128)} %copy.33) | data formatting | bytes 4194304 | tf_op jit(solution)/shard_map/all_to_all | solution.py:125
  148.3 39.6 %all_to_all.19 = f32[128,1,4096]{2,1,0:T(1,128)} all-to-all(f32[128,1,4096]{2,1,0:T(1,128)S(1)} %all_to_all.16), channel_id=1, replica_groups=mesh['grp'=4,'chan'=32] {'chan','grp'}, dimensions={0} | all-to-all | bytes 4194304 | tf_op jit(solution)/shard_map/all_to_all | solution.py:125
  187.9 2.8 %reduce_sum.9 = f32[4096]{0:T(1024)S(1)} reduce(f32[128,1,4096]{2,1,0:T(1,128)} %all_to_all.19, f32[]{:T(128)} %constant.84.clone.1), dimensions={0,1}, to_apply=%region_0.1 | reduce | flops 520192 | bytes 2113540 | tf_op jit(solution)/shard_map/reduce_sum | solution.py:126
  190.9 0.7 reshape.368
  (24 shorter events, 0.3 us)
Async XLA Ops:
  0.0 33.5 %all-to-all-start = ((bf16[128,1,16,128]{3,2,1,0:T(8,128)(2,1)}), bf16[128,1,16,128]{3,2,1,0:T(8,128)(2,1)S(1)}, u32[]{:S(2)}, u32[]{:S(2)}) async-start(bf16[128,1,16,128]{3,2,1,0:T(8,128)(2,1)} %bitcast.77), calls=%async_computation | async-start | bytes 1048576 | tf_op jit(solution)/shard_map/all_to_all | solution.py:113
  34.0 1.0 copy-start
  34.0 1.0 copy-start.1
  34.0 1.0 copy-start.2
  34.0 1.0 copy-start.3
  35.0 65.4 %copy-start.4 = (f32[16,1,256,2,128]{4,2,3,1,0:T(8,128)S(1)}, f32[16,1,256,2,128]{4,2,3,1,0:T(8,128)}, u32[]{:S(2)}) copy-start(f32[16,1,256,2,128]{4,2,3,1,0:T(8,128)} %get-tuple-element.5) | copy-start | bytes 12582916
  35.0 65.4 %copy-start.5 = (f32[16,1,256,2,128]{4,2,3,1,0:T(8,128)S(1)}, f32[16,1,256,2,128]{4,2,3,1,0:T(8,128)}, u32[]{:S(2)}) copy-start(f32[16,1,256,2,128]{4,2,3,1,0:T(8,128)} %get-tuple-element.6) | copy-start | bytes 12582916
  102.9 5.8 %copy-start.6 = (f32[32,1,128,64]{2,3,1,0:T(8,128)S(1)}, f32[32,1,128,64]{2,3,1,0:T(8,128)}, u32[]{:S(2)}) copy-start(f32[32,1,128,64]{2,3,1,0:T(8,128)} %get-tuple-element.9) | copy-start | bytes 3145732
  102.9 5.8 %copy-start.7 = (f32[32,1,128,64]{2,3,1,0:T(8,128)S(1)}, f32[32,1,128,64]{2,3,1,0:T(8,128)}, u32[]{:S(2)}) copy-start(f32[32,1,128,64]{2,3,1,0:T(8,128)} %get-tuple-element.10) | copy-start | bytes 3145732

commit v3 on v2

--- a/solution.py
+++ b/solution.py
@@ -40,13 +40,10 @@
         live = (slot < count) & (slot >= 0)
         slot_c = jnp.clip(slot, 0, SLOTS - 1)
 
-        @pl.when(live)
-        def _():
-            acc_ref[slot_c] += tile
-
+        acc_ref[slot_c] += jnp.where(live, tile, 0.0)
         return carry
 
-    lax.fori_loop(0, PAIRS, body, 0, unroll=4)
+    lax.fori_loop(0, PAIRS, body, 0, unroll=8)
     out_ref[...] = acc_ref[...].astype(out_ref.dtype)
 
 

time: 192 us -> 161 us (0.84)
  Pallas kernels: 65.4 us -> 33.9 us
    pallas_call x1, Pallas kernels: 65.4 us -> 33.9 us  [grid_slots(): pl.pallas_call(_grid_kernel, out_shape=jax.ShapeDtypeStruct((SLOTS, 2 * B...]
  transfers between devices with their start and end apart: 1 -> 1, of which waited for: 0 -> 0; matrix products, arithmetic and copies ran while one was open for 11% -> 13% of each run, Pallas kernels for 0% -> 0%
where the time goes in v3:
time: 161 us; the launch traced here: 160 us
  blocking collectives  39.5 us (25%)
  local copies, waits for them, and re-layouts  34.3 us (21%)
  Pallas kernels  33.9 us (21%)
  other arithmetic  23.4 us (15%)
  matrix products  16.5 us (10%)
  starting transfers between devices  11.5 us (7%)
    all_to_all x1, blocking collectives, body(): lax.all_to_all(send, ('chan', 'grp'), split_axis=0, concat_axis=0, tiled=...  39.5 us
    pallas_call x1, Pallas kernels, grid_slots(): pl.pallas_call(_grid_kernel, out_shape=jax.ShapeDtypeStruct((SLOTS, 2 * B...  33.9 us
    transpose x1, local copies, waits for them, and re-layouts, body(): image_t.reshape(PHASES, n_chan, rows_per, n_grp, groups_per)  12.3 us
    all_to_all x1, starting transfers between devices, body(): lax.all_to_all(direct, ('grp', 'chan'), split_axis=0, concat_axis=1, tile...  11.5 us
    all_to_all x1, local copies, waits for them, and re-layouts, body(): lax.all_to_all(send, ('chan', 'grp'), split_axis=0, concat_axis=0, tiled=...  11.4 us
    dot_general x1, matrix products, channel_image(): jnp.einsum('tclv,tcvj->tlj', summed, col_op, precision=lax.Precision.HIGH...  8.37 us
    neg x1, other arithmetic, channel_image(): -ai  8.37 us
    mul x1, local copies, waits for them, and re-layouts, channel_image(): jnp.einsum('tclv,tcvj->tlj', summed, col_op, precision=lax.Precision.HIGH...  7.55 us
  transfers between devices with their start and end apart: 1, of which 0 were waited for; matrix products, arithmetic and copies ran while one was open for 13% of the time, Pallas kernels for 0%

profile of v3, /device:TPU:1, one launch (start us, length us, event | category | flops | bytes accessed | tf_op | source)
XLA Modules:
  0.0 160.0 jit_solution(10821969319371383206)
XLA Ops:
  0.0 11.5 %all-to-all-start = ((bf16[128,1,16,128]{3,2,1,0:T(8,128)(2,1)}), bf16[128,1,16,128]{3,2,1,0:T(8,128)(2,1)S(1)}, u32[]{:S(2)}, u32[]{:S(2)}) async-start(bf16[128,1,16,128]{3,2,1,0:T(8,128)(2,1)} %bitcast.77), calls=%async_computation | async-start | bytes 1048576 | tf_op jit(solution)/shard_map/all_to_all | solution.py:110
  11.5 0.7 fusion.45
  12.2 0.7 fusion.43
  13.6 0.1 fusion.42
  13.7 1.3 copy.29
  15.0 8.4 %fusion.30 = (f32[16,256,1,128]{3,1,2,0:T(8,128)S(1)}, f32[16,256,1,128]{3,1,2,0:T(8,128)S(1)}, f32[16,256,1,128]{3,1,2,0:T(8,128)S(1)}) fusion(s32[16,128]{1,0:T(8,128)S(1)} %add_add_fusion.1, s32[256]{0:T(256)S(1)} %iota_add_fusion), kind=kLoop, calls=%fused_computation.37 | loop fusion | flops 7864320 | bytes 6300672 | tf_op jit(solution)/shard_map/neg | solution.py:88
  23.4 5.8 %fusion.31 = (f32[32,1,128,64]{2,3,1,0:T(8,128)}, f32[32,1,128,64]{2,3,1,0:T(8,128)}) fusion(s32[128]{0:T(128)S(1)} %iota_add_fusion.1, s32[32,64]{1,0:T(8,128)S(1)} %add_add_fusion), kind=kLoop, calls=%fused_computation.40 | loop fusion | flops 3932160 | bytes 2105856 | tf_op jit(solution)/shard_map/cos | solution.py:76
  29.2 4.2 %maximum_bitcast_fusion = (f32[16,1,256,2,128]{4,2,3,1,0:T(8,128)}, f32[16,1,256,2,128]{4,2,3,1,0:T(8,128)}) fusion(f32[16,256,1,128]{3,1,2,0:T(8,128)S(1)} %get-tuple-element.11, f32[16,256,1,128]{3,1,2,0:T(8,128)S(1)} %get-tuple-element.13, f32[16,256,1,128]{3,1,2,0:T(8,128)S(1)} %get-tuple-element.12), kind=kLoop, calls=%fused_computation.6 | loop fusion | flops 2097152 | bytes 14680064 | tf_op jit(solution)/shard_map/stack | solution.py:88
  33.5 0.3 copy.27
  33.8 0.2 slice_negate_fusion
  34.0 0.3 pad_maximum_fusion.1
  34.3 0.3 copy.28
  34.6 0.1 pad_maximum_fusion.w_ref
  34.8 0.3 copy-done
  35.1 33.9 %shard_map.91 = bf16[16,256,128]{2,1,0:T(8,128)(2,1)S(1)} custom-call(s32[136]{0:T(256)S(1)} %copy-done.3, s32[136]{0:T(256)S(1)} %copy-done.2, s32[136]{0:T(256)S(1)} %bitcast.71, s32[1]{0:T(128)S(6)} %copy.51.count_ref, bf16[16,128,128]{2,1,0:T(8,128)(2,1)S(1)} %bitcast.67, bf16[16,128,256]{2,1,0:T(8,128)(2,1)S(1)} %pad_maximum_fusion.w_ref, ...), custom_call_target="tpu_custom_call" | custom-call | flops 3422552064 | bytes 11534336 | tf_op jit(solution)/shard_map/pallas_call | solution.py:63
  69.0 2.3 %fusion.12 = f32[16,2,256,128]{3,2,1,0:T(8,128)S(1)} fusion(bf16[16,2,128,128,1]{3,2,1,4,0:T(8,128)(2,1)S(1)} %bitcast.68, f32[16,1,256,2,128]{4,2,3,1,0:T(8,128)S(1)} %copy-done.5, f32[16,1,256,2,128]{4,2,3,1,0:T(8,128)S(1)} %copy-done.4), kind=kOutput, calls=%fused_computation.17 | convolution fusion | flops 1612709888 | bytes 13631488 | tf_op jit(solution)/shard_map/sclku,skuv->sclv/dot_general | solution.py:89
  71.4 5.8 %fusion.9 = f32[32,2,256,128]{3,0,2,1:T(8,128)S(1)} fusion(f32[16,2,256,128]{3,2,1,0:T(8,128)S(1)} %fusion.12, f32[32,1,16,2]{0,2,3,1:T(8,128)S(1)} %get-tuple-element.15, f32[32,1,16,2]{0,2,3,1:T(8,128)S(1)} %get-tuple-element.14), kind=kOutput, calls=%fused_computation.14 | convolution fusion | flops 402655232 | bytes 12591104 | tf_op jit(solution)/shard_map/tcsk,sklv->tclv/dot_general | solution.py:95
  77.2 8.4 %bitcast_multiply_fusion = f32[32,256,64]{1,2,0:T(8,128)S(1)} fusion(f32[32,1,128,64]{2,3,1,0:T(8,128)S(1)} %copy-done.7, f32[32,1,128,64]{2,3,1,0:T(8,128)S(1)} %copy-done.6, f32[32,2,256,128]{3,0,2,1:T(8,128)S(1)} %fusion.9), kind=kOutput, calls=%fused_computation.24 | convolution fusion | flops 806354944 | bytes 12582912 | tf_op jit(solution)/shard_map/tclv,tcvj->tlj/dot_general | solution.py:102
  85.6 7.6 %copy.32 = f32[32,256,64]{0,2,1:T(8,128)} copy(f32[32,256,64]{1,2,0:T(8,128)S(1)} %bitcast_multiply_fusion) | data formatting | bytes 4194304 | tf_op jit(solution)/shard_map/mul | solution.py:102
  93.1 12.3 %copy.33 = f32[32,4,32,8,16]{4,3,2,1,0:T(8,128)} copy(f32[32,4,32,8,16]{2,4,1,3,0:T(8,128)} %bitcast.72) | data formatting | bytes 4194304 | tf_op jit(solution)/shard_map/transpose | solution.py:120
  105.4 11.4 %all_to_all.16 = f32[128,1,4096]{2,1,0:T(1,128)S(1)} reshape(f32[32,4,32,8,16]{4,3,2,1,0:T(8,128)} %copy.33) | data formatting | bytes 4194304 | tf_op jit(solution)/shard_map/all_to_all | solution.py:122
  116.8 39.5 %all_to_all.19 = f32[128,1,4096]{2,1,0:T(1,128)} all-to-all(f32[128,1,4096]{2,1,0:T(1,128)S(1)} %all_to_all.16), channel_id=1, replica_groups=mesh['grp'=4,'chan'=32] {'chan','grp'}, dimensions={0} | all-to-all | bytes 4194304 | tf_op jit(solution)/shard_map/all_to_all | solution.py:122
  156.3 2.8 %reduce_sum.9 = f32[4096]{0:T(1024)S(1)} reduce(f32[128,1,4096]{2,1,0:T(1,128)} %all_to_all.19, f32[]{:T(128)} %constant.84.clone.1), dimensions={0,1}, to_apply=%region_0.1 | reduce | flops 520192 | bytes 2113540 | tf_op jit(solution)/shard_map/reduce_sum | solution.py:123
  159.3 0.7 reshape.368
  (24 shorter events, 0.3 us)
Async XLA Ops:
  0.0 33.5 %all-to-all-start = ((bf16[128,1,16,128]{3,2,1,0:T(8,128)(2,1)}), bf16[128,1,16,128]{3,2,1,0:T(8,128)(2,1)S(1)}, u32[]{:S(2)}, u32[]{:S(2)}) async-start(bf16[128,1,16,128]{3,2,1,0:T(8,128)(2,1)} %bitcast.77), calls=%async_computation | async-start | bytes 1048576 | tf_op jit(solution)/shard_map/all_to_all | solution.py:110
  34.0 1.0 copy-start
  34.0 1.0 copy-start.1
  34.0 1.0 copy-start.2
  34.0 1.0 copy-start.3
  35.0 33.9 %copy-start.4 = (f32[16,1,256,2,128]{4,2,3,1,0:T(8,128)S(1)}, f32[16,1,256,2,128]{4,2,3,1,0:T(8,128)}, u32[]{:S(2)}) copy-start(f32[16,1,256,2,128]{4,2,3,1,0:T(8,128)} %get-tuple-element.5) | copy-start | bytes 12582916
  35.0 33.9 %copy-start.5 = (f32[16,1,256,2,128]{4,2,3,1,0:T(8,128)S(1)}, f32[16,1,256,2,128]{4,2,3,1,0:T(8,128)}, u32[]{:S(2)}) copy-start(f32[16,1,256,2,128]{4,2,3,1,0:T(8,128)} %get-tuple-element.6) | copy-start | bytes 12582916
  71.3 5.8 %copy-start.6 = (f32[32,1,128,64]{2,3,1,0:T(8,128)S(1)}, f32[32,1,128,64]{2,3,1,0:T(8,128)}, u32[]{:S(2)}) copy-start(f32[32,1,128,64]{2,3,1,0:T(8,128)} %get-tuple-element.9) | copy-start | bytes 3145732
  71.3 5.8 %copy-start.7 = (f32[32,1,128,64]{2,3,1,0:T(8,128)S(1)}, f32[32,1,128,64]{2,3,1,0:T(8,128)}, u32[]{:S(2)}) copy-start(f32[32,1,128,64]{2,3,1,0:T(8,128)} %get-tuple-element.10) | copy-start | bytes 3145732

commit v4 on v3

--- a/solution.py
+++ b/solution.py
@@ -118,9 +118,9 @@
     rows_per = ROWS // n_chan
     groups_per = CROP // PHASES // n_grp
     send = image_t.reshape(PHASES, n_chan, rows_per, n_grp, groups_per).transpose(1, 3, 0, 2, 4)
-    send = send.reshape(n_chan * n_grp, PHASES * rows_per * groups_per)
+    send = send.reshape(n_chan * n_grp, PHASES * rows_per * groups_per).astype(jnp.bfloat16)
     got = lax.all_to_all(send, ("chan", "grp"), split_axis=0, concat_axis=0, tiled=True)
-    summed = got.sum(axis=0).reshape(PHASES, rows_per, groups_per)
+    summed = got.astype(jnp.float32).sum(axis=0).reshape(PHASES, rows_per, groups_per)
     return summed.transpose(1, 2, 0).reshape(rows_per, groups_per * PHASES)
 
 

time: 161 us -> 170 us (1.056)
  matrix products: 16.5 us -> 28.1 us
  blocking collectives: 39.5 us -> 28.9 us
  other arithmetic: 23.4 us -> 30.9 us
    convert_element_type x0 -> x4, local copies, waits for them, and re-layouts: none -> 28.5 us  [body(): send.reshape(n_chan * n_grp, PHASES * rows_per * groups_per)]
    transpose x1 -> x0, local copies, waits for them, and re-layouts: 12.3 us -> none  [body(): image_t.reshape(PHASES, n_chan, rows_per, n_grp, groups_per)]
    dot_general x1, matrix products: 8.37 us -> 19.9 us  [channel_image(): jnp.einsum('tclv,tcvj->tlj', summed, col_op, precision=lax.Precision.HIGH...]
    all_to_all x1 -> x0, local copies, waits for them, and re-layouts: 11.4 us -> none  [body(): lax.all_to_all(send, ('chan', 'grp'), split_axis=0, concat_axis=0, tiled=...]
    all_to_all x1, blocking collectives: 39.5 us -> 28.9 us  [body(): lax.all_to_all(send, ('chan', 'grp'), split_axis=0, concat_axis=0, tiled=...]
    mul x1 -> x0, local copies, waits for them, and re-layouts: 7.55 us -> none  [channel_image(): jnp.einsum('tclv,tcvj->tlj', summed, col_op, precision=lax.Precision.HIGH...]
    convert_element_type x0 -> x1, other arithmetic: none -> 7.02 us  [body(): send.reshape(n_chan * n_grp, PHASES * rows_per * groups_per)]
where the time goes in v4:
time: 170 us; the launch traced here: 168 us
  Pallas kernels  34 us (20%)
  local copies, waits for them, and re-layouts  33.9 us (20%)
  other arithmetic  30.9 us (18%)
  blocking collectives  28.9 us (17%)
  matrix products  28.1 us (17%)
  starting transfers between devices  11.5 us (7%)
    pallas_call x1, Pallas kernels, grid_slots(): pl.pallas_call(_grid_kernel, out_shape=jax.ShapeDtypeStruct((SLOTS, 2 * B...  34 us
    all_to_all x1, blocking collectives, body(): lax.all_to_all(send, ('chan', 'grp'), split_axis=0, concat_axis=0, tiled=...  28.9 us
    convert_element_type x4, local copies, waits for them, and re-layouts, body(): send.reshape(n_chan * n_grp, PHASES * rows_per * groups_per)  28.5 us
    dot_general x1, matrix products, channel_image(): jnp.einsum('tclv,tcvj->tlj', summed, col_op, precision=lax.Precision.HIGH...  19.9 us
    all_to_all x1, starting transfers between devices, body(): lax.all_to_all(direct, ('grp', 'chan'), split_axis=0, concat_axis=1, tile...  11.5 us
    neg x1, other arithmetic, channel_image(): -ai  8.37 us
    convert_element_type x1, other arithmetic, body(): send.reshape(n_chan * n_grp, PHASES * rows_per * groups_per)  7.02 us
    dot_general x1, matrix products, channel_image(): jnp.einsum('tcsk,sklv->tclv', phase_op, rows_done, precision=lax.Precisio...  5.85 us
  transfers between devices with their start and end apart: 1, of which 0 were waited for; matrix products, arithmetic and copies ran while one was open for 13% of the time, Pallas kernels for 0%

profile of v4, /device:TPU:1, one launch (start us, length us, event | category | flops | bytes accessed | tf_op | source)
XLA Modules:
  0.0 168.3 jit_solution(14516934901338506986)
XLA Ops:
  0.0 11.5 %all-to-all-start = ((bf16[128,1,16,128]{3,2,1,0:T(8,128)(2,1)}), bf16[128,1,16,128]{3,2,1,0:T(8,128)(2,1)S(1)}, u32[]{:S(2)}, u32[]{:S(2)}) async-start(bf16[128,1,16,128]{3,2,1,0:T(8,128)(2,1)} %bitcast.79), calls=%async_computation | async-start | bytes 1048576 | tf_op jit(solution)/shard_map/all_to_all | solution.py:110
  11.5 0.7 fusion.46
  12.2 0.7 fusion.44
  12.8 1.3 copy.29
  15.0 8.4 %fusion.31 = (f32[16,256,1,128]{3,1,2,0:T(8,128)S(1)}, f32[16,256,1,128]{3,1,2,0:T(8,128)S(1)}, f32[16,256,1,128]{3,1,2,0:T(8,128)S(1)}) fusion(s32[16,128]{1,0:T(8,128)S(1)} %add_add_fusion.1, s32[256]{0:T(256)S(1)} %iota_add_fusion), kind=kLoop, calls=%fused_computation.39 | loop fusion | flops 7864320 | bytes 6300672 | tf_op jit(solution)/shard_map/neg | solution.py:88
  23.4 5.7 %fusion.32 = (f32[32,1,128,64]{2,3,1,0:T(8,128)S(1)}, f32[32,1,128,64]{2,3,1,0:T(8,128)}) fusion(s32[128]{0:T(128)S(1)} %iota_add_fusion.1, s32[32,64]{1,0:T(8,128)S(1)} %add_add_fusion), kind=kLoop, calls=%fused_computation.42 | loop fusion | flops 3932160 | bytes 2105856 | tf_op jit(solution)/shard_map/cos | solution.py:76
  29.1 4.2 %maximum_bitcast_fusion = (f32[16,1,256,2,128]{4,2,3,1,0:T(8,128)}, f32[16,1,256,2,128]{4,2,3,1,0:T(8,128)}) fusion(f32[16,256,1,128]{3,1,2,0:T(8,128)S(1)} %get-tuple-element.11, f32[16,256,1,128]{3,1,2,0:T(8,128)S(1)} %get-tuple-element.13, f32[16,256,1,128]{3,1,2,0:T(8,128)S(1)} %get-tuple-element.12), kind=kLoop, calls=%fused_computation.6 | loop fusion | flops 2097152 | bytes 14680064 | tf_op jit(solution)/shard_map/stack | solution.py:88
  33.5 0.3 pad_maximum_fusion.1
  33.9 1.0 copy.28
  35.2 1.2 pad_maximum_fusion.w_ref
  36.5 34.0 %shard_map.91 = bf16[16,256,128]{2,1,0:T(8,128)(2,1)S(1)} custom-call(s32[136]{0:T(256)S(1)} %copy-done.2, s32[136]{0:T(256)S(1)} %copy-done.3, s32[136]{0:T(256)S(1)} %bitcast.73, s32[1]{0:T(128)S(6)} %copy.51.count_ref, bf16[16,128,128]{2,1,0:T(8,128)(2,1)S(1)} %bitcast.69, bf16[16,128,256]{2,1,0:T(8,128)(2,1)S(1)} %pad_maximum_fusion.w_ref, ...), custom_call_target="tpu_custom_call" | custom-call | flops 3422552064 | bytes 11534336 | tf_op jit(solution)/shard_map/pallas_call | solution.py:63
  70.4 2.3 %fusion.12 = f32[16,2,256,128]{3,2,1,0:T(8,128)S(1)} fusion(bf16[16,2,128,128,1]{3,2,1,4,0:T(8,128)(2,1)S(1)} %bitcast.70, f32[16,1,256,2,128]{4,2,3,1,0:T(8,128)S(1)} %copy-done.5, f32[16,1,256,2,128]{4,2,3,1,0:T(8,128)S(1)} %copy-done.4), kind=kOutput, calls=%fused_computation.17 | convolution fusion | flops 1612709888 | bytes 13631488 | tf_op jit(solution)/shard_map/sclku,skuv->sclv/dot_general | solution.py:89
  72.8 5.9 %fusion.9 = f32[32,2,256,128]{3,0,2,1:T(8,128)S(1)} fusion(f32[16,2,256,128]{3,2,1,0:T(8,128)S(1)} %fusion.12, f32[32,1,16,2]{0,2,3,1:T(8,128)S(1)} %get-tuple-element.15, f32[32,1,16,2]{0,2,3,1:T(8,128)S(1)} %get-tuple-element.14), kind=kOutput, calls=%fused_computation.14 | convolution fusion | flops 402655232 | bytes 12591104 | tf_op jit(solution)/shard_map/tcsk,sklv->tclv/dot_general | solution.py:95
  78.7 19.9 %fusion.21 = bf16[32,256,64]{1,2,0:T(8,128)(2,1)S(1)} fusion(f32[32,1,128,64]{2,3,1,0:T(8,128)S(1)} %copy-done.6, f32[32,1,128,64]{2,3,1,0:T(8,128)S(1)} %get-tuple-element.9, f32[32,2,256,128]{3,0,2,1:T(8,128)S(1)} %fusion.9), kind=kOutput, calls=%fused_computation.25 | convolution fusion | flops 806879232 | bytes 11534336 | tf_op jit(solution)/shard_map/tclv,tcvj->tlj/dot_general | solution.py:102
  98.6 6.8 %copy.32 = bf16[32,256,64]{0,2,1:T(8,128)(2,1)} copy(bf16[32,256,64]{1,2,0:T(8,128)(2,1)S(1)} %fusion.21) | data formatting | bytes 2097152 | tf_op jit(solution)/shard_map/convert_element_type | solution.py:121
  105.4 9.0 %copy.33 = bf16[32,4,32,8,16]{4,3,2,1,0:T(8,128)(2,1)} copy(bf16[32,4,32,8,16]{2,4,1,3,0:T(8,128)(2,1)} %bitcast.74) | data formatting | bytes 2097152 | tf_op jit(solution)/shard_map/convert_element_type | solution.py:121
  114.4 12.1 %convert_element_type.84 = bf16[128,1,4096]{2,1,0:T(2,128)(2,1)S(1)} reshape(bf16[32,4,32,8,16]{4,3,2,1,0:T(8,128)(2,1)} %copy.33) | data formatting | bytes 2097152 | tf_op jit(solution)/shard_map/convert_element_type | solution.py:121
  126.5 0.5 broadcast.499
  127.0 7.0 %reduce.1 = bf16[128,4096]{1,0:T(8,128)(2,1)S(1)} reduce(bf16[128,1,4096]{2,1,0:T(2,128)(2,1)S(1)} %convert_element_type.84, bf16[]{:T(256)} %broadcast.499), dimensions={1}, to_apply=%convert_element_type.84.reduce_sub_computation | reduce | bytes 2097154 | tf_op jit(solution)/shard_map/convert_element_type | solution.py:121
  134.1 0.8 reshape.384
  134.9 28.9 %all_to_all.15 = bf16[128,2,2048]{2,1,0:T(2,128)(2,1)S(1)} all-to-all(bf16[128,2,2048]{2,1,0:T(2,128)(2,1)S(1)} %reshape.384), channel_id=1, replica_groups=mesh['grp'=4,'chan'=32] {'chan','grp'}, dimensions={0} | all-to-all | bytes 2097152 | tf_op jit(solution)/shard_map/all_to_all | solution.py:122
  163.8 1.0 reshape.385
  164.8 2.4 %convert_reduce_fusion = f32[4096]{0:T(1024)S(1)} fusion(bf16[128,1,4096]{2,1,0:T(2,128)(2,1)S(1)} %reshape.385), kind=kLoop, calls=%fused_computation.26 | loop fusion | flops 1044480 | bytes 1064960 | tf_op jit(solution)/shard_map/reduce_sum | solution.py:123
  167.4 0.7 reshape.377
  (26 shorter events, 1.0 us)
Async XLA Ops:
  0.0 33.3 %all-to-all-start = ((bf16[128,1,16,128]{3,2,1,0:T(8,128)(2,1)}), bf16[128,1,16,128]{3,2,1,0:T(8,128)(2,1)S(1)}, u32[]{:S(2)}, u32[]{:S(2)}) async-start(bf16[128,1,16,128]{3,2,1,0:T(8,128)(2,1)} %bitcast.79), calls=%async_computation | async-start | bytes 1048576 | tf_op jit(solution)/shard_map/all_to_all | solution.py:110
  33.8 2.6 %copy-start = (bf16[1,16,128,128]{3,2,1,0:T(8,128)(2,1)S(1)}, bf16[1,16,128,128]{3,2,1,0:T(8,128)(2,1)}, u32[]{:S(2)}) copy-start(bf16[1,16,128,128]{3,2,1,0:T(8,128)(2,1)} %param.11) | copy-start | bytes 1572868
  33.9 2.6 %copy-start.1 = (s32[1,136]{1,0:T(1,128)S(1)}, s32[1,136]{1,0:T(1,128)}, u32[]{:S(2)}) copy-start(s32[1,136]{1,0:T(1,128)} %param.13) | copy-start | bytes 1636
  33.9 2.6 %copy-start.2 = (s32[136]{0:T(256)S(1)}, s32[136]{0:T(256)}, u32[]{:S(2)}) copy-start(s32[136]{0:T(256)} %constant.85.clone.ptab) | copy-start | bytes 1636
  33.9 2.5 %copy-start.3 = (s32[136]{0:T(256)S(1)}, s32[136]{0:T(256)}, u32[]{:S(2)}) copy-start(s32[136]{0:T(256)} %constant.86.clone.qtab) | copy-start | bytes 1636
  36.4 34.0 %copy-start.4 = (f32[16,1,256,2,128]{4,2,3,1,0:T(8,128)S(1)}, f32[16,1,256,2,128]{4,2,3,1,0:T(8,128)}, u32[]{:S(2)}) copy-start(f32[16,1,256,2,128]{4,2,3,1,0:T(8,128)} %get-tuple-element.5) | copy-start | bytes 12582916
  36.4 34.0 %copy-start.5 = (f32[16,1,256,2,128]{4,2,3,1,0:T(8,128)S(1)}, f32[16,1,256,2,128]{4,2,3,1,0:T(8,128)}, u32[]{:S(2)}) copy-start(f32[16,1,256,2,128]{4,2,3,1,0:T(8,128)} %get-tuple-element.6) | copy-start | bytes 12582916
  72.8 5.9 %copy-start.6 = (f32[32,1,128,64]{2,3,1,0:T(8,128)S(1)}, f32[32,1,128,64]{2,3,1,0:T(8,128)}, u32[]{:S(2)}) copy-start(f32[32,1,128,64]{2,3,1,0:T(8,128)} %get-tuple-element.10) | copy-start | bytes 3145732

commit v5 on v4

--- a/solution.py
+++ b/solution.py
@@ -93,14 +93,17 @@
     zr, zi = _cos_sin(jnp.mod(phases[:, None] * block_cols[None, :], PHASES), PHASES)
     phase_op = jnp.stack([jnp.stack([zr, -zi], axis=2), jnp.stack([zi, zr], axis=2)], axis=1)
     summed = jnp.einsum(
-        "tcsk,sklv->tclv", phase_op, rows_done, precision=lax.Precision.HIGH, preferred_element_type=jnp.float32
+        "tcsk,sklv->ltcv", phase_op, rows_done, precision=lax.Precision.HIGH, preferred_element_type=jnp.float32
     )
+    dr, di = _cos_sin(jnp.mod((phases[:, None] - GRID // 4) * offsets[None, :] - (GRID // 2) * phases[:, None], GRID), GRID)
+    turned_r = summed[:, :, 0] * dr - summed[:, :, 1] * di
+    turned_i = summed[:, :, 0] * di + summed[:, :, 1] * dr
+    turned = jnp.stack([turned_r, turned_i], axis=2)
     col_groups = jnp.arange(CROP // PHASES, dtype=jnp.int32)
-    pixel_cols = col_groups[None, :] * PHASES + phases[:, None] - CROP // 2
-    br, bi = _cos_sin(jnp.mod(pixel_cols[:, None, :] * (offsets - GRID // 2)[None, :, None], GRID), GRID)
-    col_op = jnp.stack([br, -bi], axis=1)
+    gr, gi = _cos_sin(jnp.mod(offsets[:, None] * col_groups[None, :], BLOCK), BLOCK)
+    col_op = jnp.stack([gr, -gi], axis=0)
     return jnp.einsum(
-        "tclv,tcvj->tlj", summed, col_op, precision=lax.Precision.HIGH, preferred_element_type=jnp.float32
+        "cvj,ltcv->jlt", col_op, turned, precision=lax.Precision.HIGH, preferred_element_type=jnp.float32
     ) * (1.0 / GRID)
 
 
@@ -117,11 +120,11 @@
     n_grp = lax.axis_size("grp")
     rows_per = ROWS // n_chan
     groups_per = CROP // PHASES // n_grp
-    send = image_t.reshape(PHASES, n_chan, rows_per, n_grp, groups_per).transpose(1, 3, 0, 2, 4)
-    send = send.reshape(n_chan * n_grp, PHASES * rows_per * groups_per).astype(jnp.bfloat16)
-    got = lax.all_to_all(send, ("chan", "grp"), split_axis=0, concat_axis=0, tiled=True)
-    summed = got.astype(jnp.float32).sum(axis=0).reshape(PHASES, rows_per, groups_per)
-    return summed.transpose(1, 2, 0).reshape(rows_per, groups_per * PHASES)
+    send = image_t.reshape(n_grp, groups_per, n_chan, rows_per * PHASES).transpose(0, 2, 1, 3)
+    send = send.reshape(n_grp * n_chan, groups_per, rows_per * PHASES).astype(jnp.bfloat16)
+    got = lax.all_to_all(send, ("grp", "chan"), split_axis=0, concat_axis=0, tiled=True)
+    summed = got.astype(jnp.float32).sum(axis=0).reshape(groups_per, rows_per, PHASES)
+    return summed.transpose(1, 0, 2).reshape(rows_per, groups_per * PHASES)
 
 
 def solution(mesh):

time: 170 us -> 121 us (0.71); the launches traced: 168 us -> 121 us
  local copies, waits for them, and re-layouts: 33.9 us -> 11.9 us
  other arithmetic: 30.9 us -> 17.9 us
  matrix products: 28.1 us -> 16.3 us
    convert_element_type x4 -> x3, local copies, waits for them, and re-layouts: 28.5 us -> 9.19 us  [body(): send.reshape(n_grp * n_chan, groups_per, rows_per * PHASES)]
    dot_general x2, matrix products: 25.7 us -> 14 us  [the longest x1 8.18 us: channel_image(): jnp.einsum('cvj,ltcv->jlt', col_op, turned, precision=lax.Precision.HIGH,...]
    convert_element_type x1 -> x0, other arithmetic: 7.02 us -> none  [body(): send.reshape(n_chan * n_grp, PHASES * rows_per * groups_per)]
    cos x1, other arithmetic: 5.65 us -> 0.15 us  [_cos_sin(): return (jnp.cos(angles), jnp.sin(angles))]
    reduce_sum x1, other arithmetic: 2.4 us -> 0.19 us  [body(): got.astype(jnp.float32).sum(axis=0).reshape(groups_per, rows_per, PHASES)]
    unnamed x17 -> x13, local copies, waits for them, and re-layouts: 3.2 us -> 1.34 us
where the time goes in v5:
time: 121 us
  Pallas kernels  33.9 us (28%)
  blocking collectives  28.7 us (24%)
  other arithmetic  17.9 us (15%)
  matrix products  16.3 us (13%)
  local copies, waits for them, and re-layouts  11.9 us (10%)
  starting transfers between devices  11.5 us (10%)
    pallas_call x1, Pallas kernels, grid_slots(): pl.pallas_call(_grid_kernel, out_shape=jax.ShapeDtypeStruct((SLOTS, 2 * B...  33.9 us
    all_to_all x1, blocking collectives, body(): lax.all_to_all(send, ('grp', 'chan'), split_axis=0, concat_axis=0, tiled=...  28.7 us
    all_to_all x1, starting transfers between devices, body(): lax.all_to_all(direct, ('grp', 'chan'), split_axis=0, concat_axis=1, tile...  11.5 us
    convert_element_type x3, local copies, waits for them, and re-layouts, body(): send.reshape(n_grp * n_chan, groups_per, rows_per * PHASES)  9.19 us
    neg x1, other arithmetic, channel_image(): -ai  8.37 us
    dot_general x1, matrix products, channel_image(): jnp.einsum('cvj,ltcv->jlt', col_op, turned, precision=lax.Precision.HIGH,...  8.18 us
    dot_general x1, matrix products, channel_image(): jnp.einsum('tcsk,sklv->ltcv', phase_op, rows_done, precision=lax.Precisio...  5.78 us
    another operation x1, other arithmetic, channel_image(): jnp.stack([jnp.stack([ar, -ai], axis=2), jnp.stack([ai, ar], axis=2)], ax...  4.23 us
  transfers between devices with their start and end apart: 1, of which 0 were waited for; matrix products, arithmetic and copies ran while one was open for 13% of the time, Pallas kernels for 0%

profile of v5, /device:TPU:1, one launch (start us, length us, event | category | flops | bytes accessed | tf_op | source)
XLA Modules:
  0.0 121.1 jit_solution(3073774500076311038)
XLA Ops:
  0.0 11.5 %all-to-all-start = ((bf16[128,1,16,128]{3,2,1,0:T(8,128)(2,1)}), bf16[128,1,16,128]{3,2,1,0:T(8,128)(2,1)S(1)}, u32[]{:S(2)}, u32[]{:S(2)}) async-start(bf16[128,1,16,128]{3,2,1,0:T(8,128)(2,1)} %bitcast.76), calls=%async_computation | async-start | bytes 1048576 | tf_op jit(solution)/shard_map/all_to_all | solution.py:113
  11.5 0.7 fusion.50
  12.2 0.7 fusion.48
  12.8 0.1 sine_negate_fusion
  13.0 1.3 %copy.31 = bf16[1,16,128,128]{2,3,1,0:T(8,128)(2,1)S(1)} copy(bf16[1,16,128,128]{3,2,1,0:T(8,128)(2,1)} %param.12) | data formatting | bytes 1048576 | tf_op args[3]
  15.2 8.4 %fusion.22 = (f32[16,256,1,128]{3,1,2,0:T(8,128)S(1)}, f32[16,256,1,128]{3,1,2,0:T(8,128)S(1)}, f32[16,256,1,128]{3,1,2,0:T(8,128)S(1)}) fusion(s32[16,128]{1,0:T(8,128)S(1)} %add_add_fusion, s32[256]{0:T(256)S(1)} %iota_add_fusion), kind=kLoop, calls=%fused_computation.29 | loop fusion | flops 7864320 | bytes 6300672 | tf_op jit(solution)/shard_map/neg | solution.py:88
  23.6 0.2 fusion.38
  23.7 4.2 %maximum_bitcast_fusion = (f32[16,1,256,2,128]{4,2,3,1,0:T(8,128)}, f32[16,1,256,2,128]{4,2,3,1,0:T(8,128)}) fusion(f32[16,256,1,128]{3,1,2,0:T(8,128)S(1)} %get-tuple-element.11, f32[16,256,1,128]{3,1,2,0:T(8,128)S(1)} %get-tuple-element.13, f32[16,256,1,128]{3,1,2,0:T(8,128)S(1)} %get-tuple-element.12), kind=kLoop, calls=%fused_computation.7 | loop fusion | flops 2097152 | bytes 14680064 | tf_op jit(solution)/shard_map/stack | solution.py:88
  28.0 0.2 slice_negate_fusion
  28.2 0.3 pad_maximum_fusion.2
  28.5 0.3 copy.30
  28.8 0.3 copy.29
  29.3 33.9 %shard_map.91 = bf16[16,256,128]{2,1,0:T(8,128)(2,1)S(1)} custom-call(s32[136]{0:T(256)S(1)} %copy-done.3, s32[136]{0:T(256)S(1)} %copy-done.2, s32[136]{0:T(256)S(1)} %bitcast.70, s32[1]{0:T(128)S(6)} %copy.52.count_ref, bf16[16,128,128]{2,1,0:T(8,128)(2,1)S(1)} %bitcast.66, bf16[16,128,256]{2,1,0:T(8,128)(2,1)S(1)} %pad_maximum_fusion.1.w_ref, ...), custom_call_target="tpu_custom_call" | custom-call | flops 3422552064 | bytes 11534336 | tf_op jit(solution)/shard_map/pallas_call | solution.py:63
  63.2 2.3 %fusion.11 = f32[16,2,256,128,1]{3,2,1,0,4:T(8,128)S(1)} fusion(bf16[16,2,128,128,1]{3,2,1,4,0:T(8,128)(2,1)S(1)} %bitcast.67, f32[16,1,256,2,128]{4,2,3,1,0:T(8,128)S(1)} %copy-done.5, f32[16,1,256,2,128]{4,2,3,1,0:T(8,128)S(1)} %copy-done.4), kind=kOutput, calls=%fused_computation.19 | convolution fusion | flops 1612709888 | bytes 13631488 | tf_op jit(solution)/shard_map/sclku,skuv->sclv/dot_general | solution.py:89
  65.6 5.8 %fusion.8 = f32[256,32,2,128]{3,1,2,0:T(8,128)S(1)} fusion(f32[16,2,256,128,1]{3,2,1,0,4:T(8,128)S(1)} %fusion.11, f32[32,1,16,2]{0,2,3,1:T(8,128)S(1)} %get-tuple-element.15, f32[32,1,16,2]{0,2,3,1:T(8,128)S(1)} %get-tuple-element.14), kind=kOutput, calls=%fused_computation.16 | convolution fusion | flops 402655232 | bytes 12591104 | tf_op jit(solution)/shard_map/tcsk,sklv->ltcv/dot_general | solution.py:95
  71.4 1.4 %multiply_subtract_fusion = (f32[256,32,1,128]{3,1,2,0:T(8,128)S(1)}, f32[256,32,1,128]{3,1,2,0:T(8,128)S(1)}) fusion(f32[256,32,2,128]{3,1,2,0:T(8,128)S(1)} %fusion.8, f32[32,128]{1,0:T(8,128)S(1)} %get-tuple-element.17, f32[32,128]{1,0:T(8,128)S(1)} %get-tuple-element.16), kind=kLoop, calls=%fused_computation.12 | loop fusion | flops 6291456 | bytes 16809984 | tf_op jit(solution)/shard_map/sub | solution.py:99
  72.7 1.2 %pad_maximum_fusion = f32[256,32,2,128]{3,1,2,0:T(8,128)S(1)} fusion(f32[256,32,1,128]{3,1,2,0:T(8,128)S(1)} %get-tuple-element.6, f32[256,32,1,128]{3,1,2,0:T(8,128)S(1)} %get-tuple-element.5), kind=kLoop, calls=%fused_computation.4 | loop fusion | flops 2097152 | bytes 16777216 | tf_op jit(solution)/shard_map/stack | solution.py:101
  74.0 8.2 %fusion.17 = bf16[64,256,32]{1,0,2:T(8,128)(2,1)S(1)} fusion(f32[256,32,2,128]{3,1,2,0:T(8,128)S(1)} %pad_maximum_fusion, f32[1,128,64]{1,2,0:T(8,128)S(1)} %get-tuple-element.23, f32[1,128,64]{1,2,0:T(8,128)S(1)} %get-tuple-element.24), kind=kOutput, calls=%fused_computation.24 | convolution fusion | flops 806371328 | bytes 9502720 | tf_op jit(solution)/shard_map/cvj,ltcv->jlt/dot_general | solution.py:105
  82.1 3.3 %copy.34 = bf16[64,256,32]{2,1,0:T(8,128)(2,1)} copy(bf16[64,256,32]{1,0,2:T(8,128)(2,1)S(1)} %fusion.17) | data formatting | bytes 2097152 | tf_op jit(solution)/shard_map/convert_element_type | solution.py:124
  85.4 5.3 %convert_element_type.89 = bf16[4,16,32,256]{3,2,1,0:T(8,128)(2,1)S(1)} reshape(bf16[64,256,32]{2,1,0:T(8,128)(2,1)} %copy.34) | data formatting | bytes 2097152 | tf_op jit(solution)/shard_map/convert_element_type | solution.py:124
  90.7 0.6 copy.35
  91.3 28.7 %all_to_all.14 = bf16[128,16,256]{2,1,0:T(8,128)(2,1)S(1)} all-to-all(bf16[128,16,256]{2,1,0:T(8,128)(2,1)S(1)} %bitcast.72), channel_id=1, replica_groups=mesh['grp'=4,'chan'=32] {'grp','chan'}, dimensions={0} | all-to-all | bytes 2097152 | tf_op jit(solution)/shard_map/all_to_all | solution.py:125
  120.1 0.2 convert_reduce_fusion
  120.4 0.7 reshape.443
  (21 shorter events, 0.5 us)
Async XLA Ops:
  0.0 28.0 %all-to-all-start = ((bf16[128,1,16,128]{3,2,1,0:T(8,128)(2,1)}), bf16[128,1,16,128]{3,2,1,0:T(8,128)(2,1)S(1)}, u32[]{:S(2)}, u32[]{:S(2)}) async-start(bf16[128,1,16,128]{3,2,1,0:T(8,128)(2,1)} %bitcast.76), calls=%async_computation | async-start | bytes 1048576 | tf_op jit(solution)/shard_map/all_to_all | solution.py:113
  27.9 1.3 %copy-start = (bf16[1,16,128,128]{3,2,1,0:T(8,128)(2,1)S(1)}, bf16[1,16,128,128]{3,2,1,0:T(8,128)(2,1)}, u32[]{:S(2)}) copy-start(bf16[1,16,128,128]{3,2,1,0:T(8,128)(2,1)} %param.11) | copy-start | bytes 1572868
  27.9 1.3 %copy-start.1 = (s32[1,136]{1,0:T(1,128)S(1)}, s32[1,136]{1,0:T(1,128)}, u32[]{:S(2)}) copy-start(s32[1,136]{1,0:T(1,128)} %param.13) | copy-start | bytes 1636
  28.0 1.3 %copy-start.2 = (s32[136]{0:T(256)S(1)}, s32[136]{0:T(256)}, u32[]{:S(2)}) copy-start(s32[136]{0:T(256)} %constant.100.clone.qtab) | copy-start | bytes 1636
  28.0 1.3 %copy-start.3 = (s32[136]{0:T(256)S(1)}, s32[136]{0:T(256)}, u32[]{:S(2)}) copy-start(s32[136]{0:T(256)} %constant.99.clone.ptab) | copy-start | bytes 1636
  29.3 33.9 %copy-start.4 = (f32[16,1,256,2,128]{4,2,3,1,0:T(8,128)S(1)}, f32[16,1,256,2,128]{4,2,3,1,0:T(8,128)}, u32[]{:S(2)}) copy-start(f32[16,1,256,2,128]{4,2,3,1,0:T(8,128)} %get-tuple-element.7) | copy-start | bytes 12582916
  29.3 33.9 %copy-start.5 = (f32[16,1,256,2,128]{4,2,3,1,0:T(8,128)S(1)}, f32[16,1,256,2,128]{4,2,3,1,0:T(8,128)}, u32[]{:S(2)}) copy-start(f32[16,1,256,2,128]{4,2,3,1,0:T(8,128)} %get-tuple-element.8) | copy-start | bytes 12582916

commit v6 on v5

--- a/solution.py
+++ b/solution.py
@@ -83,8 +83,10 @@
     block_cols = blocks_here % per_side
     offsets = jnp.arange(BLOCK, dtype=jnp.int32)
     pixel_rows = jnp.arange(ROWS, dtype=jnp.int32) - ROWS // 2
-    grid_rows = block_rows[:, None] * BLOCK + offsets[None, :] - GRID // 2
-    ar, ai = _cos_sin(jnp.mod(pixel_rows[None, :, None] * grid_rows[:, None, :], GRID), GRID)
+    er, ei = _cos_sin(jnp.mod(block_rows[:, None] * pixel_rows[None, :], PHASES), PHASES)
+    br0, bi0 = _cos_sin(jnp.mod(pixel_rows[:, None] * (offsets - GRID // 2)[None, :], GRID), GRID)
+    ar = er[:, :, None] * br0[None] - ei[:, :, None] * bi0[None]
+    ai = er[:, :, None] * bi0[None] + ei[:, :, None] * br0[None]
     row_op = jnp.stack([jnp.stack([ar, -ai], axis=2), jnp.stack([ai, ar], axis=2)], axis=1)
     rows_done = jnp.einsum(
         "sclku,skuv->sclv", row_op, grids, precision=lax.Precision.HIGH, preferred_element_type=jnp.float32
@@ -102,9 +104,14 @@
     col_groups = jnp.arange(CROP // PHASES, dtype=jnp.int32)
     gr, gi = _cos_sin(jnp.mod(offsets[:, None] * col_groups[None, :], BLOCK), BLOCK)
     col_op = jnp.stack([gr, -gi], axis=0)
-    return jnp.einsum(
-        "cvj,ltcv->jlt", col_op, turned, precision=lax.Precision.HIGH, preferred_element_type=jnp.float32
-    ) * (1.0 / GRID)
+    image = lax.dot_general(
+        col_op.reshape(2 * BLOCK, CROP // PHASES),
+        turned.reshape(ROWS * PHASES, 2 * BLOCK),
+        (((0,), (1,)), ((), ())),
+        precision=lax.Precision.HIGH,
+        preferred_element_type=jnp.float32,
+    )
+    return (image * (1.0 / GRID)).reshape(CROP // PHASES, ROWS, PHASES)
 
 
 def body(voltages, model_vis, kernel_u, kernel_v, pair_slot, slot_block, slot_count):

time: 121 us -> 110 us (0.909)
  other arithmetic: 17.9 us -> 11.5 us
  matrix products: 16.3 us -> 12.5 us
  waiting for transfers between devices: 0.01 us -> 3.78 us
  blocking collectives: 28.7 us -> 25 us
    convert_element_type x3 -> x1, local copies, waits for them, and re-layouts: 9.19 us -> 0.59 us  [body(): send.reshape(n_grp * n_chan, groups_per, rows_per * PHASES)]
    another operation x0 -> x1, local copies, waits for them, and re-layouts: none -> 7.36 us  [channel_image(): turned = jnp.stack([turned_r, turned_i], axis=2)]
    neg x1, other arithmetic: 8.37 us -> 1.15 us  [channel_image(): -ai]
    dot_general x1, matrix products: 8.18 us -> 4.34 us  [channel_image(): lax.dot_general(col_op.reshape(2 * BLOCK, CROP // PHASES), turned.reshape...]
    all_to_all x1, waiting for transfers between devices: 0.01 us -> 3.78 us  [body(): lax.all_to_all(direct, ('grp', 'chan'), split_axis=0, concat_axis=1, tile...]
    all_to_all x1, blocking collectives: 28.7 us -> 25 us  [body(): lax.all_to_all(send, ('grp', 'chan'), split_axis=0, concat_axis=0, tiled=...]
  transfers between devices with their start and end apart: 1 -> 1, of which waited for: 0 -> 1; matrix products, arithmetic and copies ran while one was open for 13% -> 9% of each run, Pallas kernels for 0% -> 0%
where the time goes in v6:
time: 110 us
  Pallas kernels  33.9 us (31%)
  blocking collectives  25 us (23%)
  matrix products  12.5 us (11%)
  starting transfers between devices  11.5 us (10%)
  other arithmetic  11.5 us (10%)
  local copies, waits for them, and re-layouts  10.9 us (10%)
  waiting for transfers between devices  3.78 us (3%)
    pallas_call x1, Pallas kernels, grid_slots(): pl.pallas_call(_grid_kernel, out_shape=jax.ShapeDtypeStruct((SLOTS, 2 * B...  33.9 us
    all_to_all x1, blocking collectives, body(): lax.all_to_all(send, ('grp', 'chan'), split_axis=0, concat_axis=0, tiled=...  25 us
    all_to_all x1, starting transfers between devices, body(): lax.all_to_all(direct, ('grp', 'chan'), split_axis=0, concat_axis=1, tile...  11.5 us
    another operation x1, local copies, waits for them, and re-layouts, channel_image(): turned = jnp.stack([turned_r, turned_i], axis=2)  7.36 us
    dot_general x1, matrix products, channel_image(): jnp.einsum('tcsk,sklv->ltcv', phase_op, rows_done, precision=lax.Precisio...  5.78 us
    dot_general x1, matrix products, channel_image(): lax.dot_general(col_op.reshape(2 * BLOCK, CROP // PHASES), turned.reshape...  4.34 us
    another operation x1, other arithmetic, channel_image(): jnp.stack([jnp.stack([ar, -ai], axis=2), jnp.stack([ai, ar], axis=2)], ax...  4.24 us
    all_to_all x1, waiting for transfers between devices, body(): lax.all_to_all(direct, ('grp', 'chan'), split_axis=0, concat_axis=1, tile...  3.78 us
  transfers between devices with their start and end apart: 1, of which 1 were waited for; matrix products, arithmetic and copies ran while one was open for 9% of the time, Pallas kernels for 0%

profile of v6, /device:TPU:1, one launch (start us, length us, event | category | flops | bytes accessed | tf_op | source)
XLA Modules:
  0.0 110.0 jit_solution(8815857814914803548)
XLA Ops:
  0.0 11.5 %all-to-all-start = ((bf16[128,1,16,128]{3,2,1,0:T(8,128)(2,1)}), bf16[128,1,16,128]{3,2,1,0:T(8,128)(2,1)S(1)}, u32[]{:S(2)}, u32[]{:S(2)}) async-start(bf16[128,1,16,128]{3,2,1,0:T(8,128)(2,1)} %bitcast.80), calls=%async_computation | async-start | bytes 1048576 | tf_op jit(solution)/shard_map/all_to_all | solution.py:120
  11.5 0.7 and_select_fusion.1
  12.2 0.7 fusion.49
  12.8 0.3 sine_negate_fusion
  13.1 0.6 fusion.23
  13.9 1.3 %copy.28 = bf16[1,16,128,128]{2,3,1,0:T(8,128)(2,1)S(1)} copy(bf16[1,16,128,128]{3,2,1,0:T(8,128)(2,1)} %param.12) | data formatting | bytes 1048576 | tf_op args[3]
  16.0 1.1 %fusion.15 = (f32[16,256,1,128]{3,1,2,0:T(8,128)S(1)}, f32[16,256,1,128]{3,1,2,0:T(8,128)S(1)}, f32[16,256,1,128]{3,1,2,0:T(8,128)S(1)}) fusion(f32[256,128]{1,0:T(8,128)S(1)} %get-tuple-element.18, f32[16,256]{1,0:T(8,128)S(1)} %get-tuple-element.17, f32[256,128]{1,0:T(8,128)S(1)} %get-tuple-element.19, f32[16,256]{1,0:T(8,128)S(1)} %get-tuple-element.16), kind=kLoop, calls=%fused_computation.23 | loop fusion | flops 3670016 | bytes 6586368 | tf_op jit(solution)/shard_map/neg | solution.py:90
  17.3 4.2 %maximum_bitcast_fusion = (f32[16,1,256,2,128]{4,2,3,1,0:T(8,128)}, f32[16,1,256,2,128]{4,2,3,1,0:T(8,128)}) fusion(f32[16,256,1,128]{3,1,2,0:T(8,128)S(1)} %get-tuple-element.11, f32[16,256,1,128]{3,1,2,0:T(8,128)S(1)} %get-tuple-element.13, f32[16,256,1,128]{3,1,2,0:T(8,128)S(1)} %get-tuple-element.12), kind=kLoop, calls=%fused_computation.9 | loop fusion | flops 2097152 | bytes 14680064 | tf_op jit(solution)/shard_map/stack | solution.py:90
  21.6 3.8 %all-to-all-done = bf16[128,1,16,128]{3,2,1,0:T(8,128)(2,1)S(1)} async-done(((bf16[128,1,16,128]{3,2,1,0:T(8,128)(2,1)}), bf16[128,1,16,128]{3,2,1,0:T(8,128)(2,1)S(1)}, u32[]{:S(2)}, u32[]{:S(2)}) %all-to-all-start) | async-done | bytes 524320 | tf_op jit(solution)/shard_map/all_to_all | solution.py:120
  25.4 0.2 slice_negate_fusion
  25.6 0.3 pad_maximum_fusion.2
  25.9 0.3 copy.27
  26.2 0.3 copy.26
  26.7 33.9 %shard_map.91 = bf16[16,256,128]{2,1,0:T(8,128)(2,1)S(1)} custom-call(s32[136]{0:T(256)S(1)} %copy-done.2, s32[136]{0:T(256)S(1)} %copy-done.3, s32[136]{0:T(256)S(1)} %bitcast.71, s32[1]{0:T(128)S(6)} %copy.49.count_ref, bf16[16,128,128]{2,1,0:T(8,128)(2,1)S(1)} %bitcast.67, bf16[16,128,256]{2,1,0:T(8,128)(2,1)S(1)} %pad_maximum_fusion.1.w_ref, ...), custom_call_target="tpu_custom_call" | custom-call | flops 3422552064 | bytes 11534336 | tf_op jit(solution)/shard_map/pallas_call | solution.py:63
  60.6 2.4 %fusion.12 = f32[16,2,256,128,1]{3,2,1,0,4:T(8,128)S(1)} fusion(bf16[16,2,128,128,1]{3,2,1,4,0:T(8,128)(2,1)S(1)} %bitcast.68, f32[16,1,256,2,128]{4,2,3,1,0:T(8,128)S(1)} %copy-done.5, f32[16,1,256,2,128]{4,2,3,1,0:T(8,128)S(1)} %copy-done.4), kind=kOutput, calls=%fused_computation.16 | convolution fusion | flops 1612709888 | bytes 13631488 | tf_op jit(solution)/shard_map/sclku,skuv->sclv/dot_general | solution.py:91
  63.0 5.8 %fusion.9 = f32[256,32,2,128]{3,1,2,0:T(8,128)S(1)} fusion(f32[16,2,256,128,1]{3,2,1,0,4:T(8,128)S(1)} %fusion.12, f32[32,1,16,2]{0,2,3,1:T(8,128)S(1)} %get-tuple-element.15, f32[32,1,16,2]{0,2,3,1:T(8,128)S(1)} %get-tuple-element.14), kind=kOutput, calls=%fused_computation.15 | convolution fusion | flops 402655232 | bytes 12591104 | tf_op jit(solution)/shard_map/tcsk,sklv->ltcv/dot_general | solution.py:97
  68.8 1.3 %multiply_subtract_fusion = (f32[256,32,1,128]{3,1,2,0:T(8,128)S(1)}, f32[256,32,1,128]{3,1,2,0:T(8,128)S(1)}) fusion(f32[256,32,2,128]{3,1,2,0:T(8,128)S(1)} %fusion.9, f32[32,128]{1,0:T(8,128)S(1)} %get-tuple-element.21, f32[32,128]{1,0:T(8,128)S(1)} %get-tuple-element.20), kind=kLoop, calls=%fused_computation.14 | loop fusion | flops 6291456 | bytes 16809984 | tf_op jit(solution)/shard_map/sub | solution.py:101
  70.2 1.2 %pad_maximum_fusion = f32[256,32,2,128]{3,1,2,0:T(8,128)S(1)} fusion(f32[256,32,1,128]{3,1,2,0:T(8,128)S(1)} %get-tuple-element.6, f32[256,32,1,128]{3,1,2,0:T(8,128)S(1)} %get-tuple-element.5), kind=kLoop, calls=%fused_computation.8 | loop fusion | flops 2097152 | bytes 16777216 | tf_op jit(solution)/shard_map/stack | solution.py:103
  71.4 7.4 %copy.30 = f32[256,32,2,128]{3,2,1,0:T(2,128)S(1)} copy(f32[256,32,2,128]{3,1,2,0:T(8,128)S(1)} %pad_maximum_fusion) | data formatting | bytes 16777216 | tf_op jit(solution)/shard_map/stack | solution.py:103
  78.8 4.3 %fusion = bf16[64,8192]{1,0:T(8,128)(2,1)S(1)} fusion(f32[256,64]{1,0:T(8,128)S(1)} %bitcast.79, f32[1024,8,2,128]{3,2,1,0:T(2,128)S(1)} %bitcast.72), kind=kOutput, calls=%fused_computation.1 | convolution fusion | flops 806354944 | bytes 9502720 | tf_op jit(solution)/shard_map/dot_general | solution.py:107
  83.1 0.3 copy.40
  83.4 0.6 copy.31
  84.0 25.0 %all_to_all.14 = bf16[128,16,256]{2,1,0:T(8,128)(2,1)S(1)} all-to-all(bf16[128,16,256]{2,1,0:T(8,128)(2,1)S(1)} %bitcast.75), channel_id=1, replica_groups=mesh['grp'=4,'chan'=32] {'grp','chan'}, dimensions={0} | all-to-all | bytes 2097152 | tf_op jit(solution)/shard_map/all_to_all | solution.py:132
  109.3 0.7 reshape.544
  (24 shorter events, 0.9 us)
Async XLA Ops:
  0.0 25.4 %all-to-all-start = ((bf16[128,1,16,128]{3,2,1,0:T(8,128)(2,1)}), bf16[128,1,16,128]{3,2,1,0:T(8,128)(2,1)S(1)}, u32[]{:S(2)}, u32[]{:S(2)}) async-start(bf16[128,1,16,128]{3,2,1,0:T(8,128)(2,1)} %bitcast.80), calls=%async_computation | async-start | bytes 1048576 | tf_op jit(solution)/shard_map/all_to_all | solution.py:120
  21.6 5.1 %copy-start = (bf16[1,16,128,128]{3,2,1,0:T(8,128)(2,1)S(1)}, bf16[1,16,128,128]{3,2,1,0:T(8,128)(2,1)}, u32[]{:S(2)}) copy-start(bf16[1,16,128,128]{3,2,1,0:T(8,128)(2,1)} %param.11) | copy-start | bytes 1572868
  21.6 5.1 %copy-start.1 = (s32[1,136]{1,0:T(1,128)S(1)}, s32[1,136]{1,0:T(1,128)}, u32[]{:S(2)}) copy-start(s32[1,136]{1,0:T(1,128)} %param.13) | copy-start | bytes 1636
  21.6 5.1 %copy-start.2 = (s32[136]{0:T(256)S(1)}, s32[136]{0:T(256)}, u32[]{:S(2)}) copy-start(s32[136]{0:T(256)} %constant.107.clone.ptab) | copy-start | bytes 1636
  21.6 5.1 %copy-start.3 = (s32[136]{0:T(256)S(1)}, s32[136]{0:T(256)}, u32[]{:S(2)}) copy-start(s32[136]{0:T(256)} %constant.108.clone.qtab) | copy-start | bytes 1636
  26.7 33.9 %copy-start.4 = (f32[16,1,256,2,128]{4,2,3,1,0:T(8,128)S(1)}, f32[16,1,256,2,128]{4,2,3,1,0:T(8,128)}, u32[]{:S(2)}) copy-start(f32[16,1,256,2,128]{4,2,3,1,0:T(8,128)} %get-tuple-element.7) | copy-start | bytes 12582916
  26.7 33.9 %copy-start.5 = (f32[16,1,256,2,128]{4,2,3,1,0:T(8,128)S(1)}, f32[16,1,256,2,128]{4,2,3,1,0:T(8,128)}, u32[]{:S(2)}) copy-start(f32[16,1,256,2,128]{4,2,3,1,0:T(8,128)} %get-tuple-element.8) | copy-start | bytes 12582916

commit v7 on v6

--- a/solution.py
+++ b/solution.py
@@ -43,7 +43,7 @@
         acc_ref[slot_c] += jnp.where(live, tile, 0.0)
         return carry
 
-    lax.fori_loop(0, PAIRS, body, 0, unroll=8)
+    lax.fori_loop(0, PAIRS, body, 0, unroll=17)
     out_ref[...] = acc_ref[...].astype(out_ref.dtype)
 
 
@@ -100,12 +100,12 @@
     dr, di = _cos_sin(jnp.mod((phases[:, None] - GRID // 4) * offsets[None, :] - (GRID // 2) * phases[:, None], GRID), GRID)
     turned_r = summed[:, :, 0] * dr - summed[:, :, 1] * di
     turned_i = summed[:, :, 0] * di + summed[:, :, 1] * dr
-    turned = jnp.stack([turned_r, turned_i], axis=2)
+    turned = jnp.concatenate([turned_r, turned_i], axis=2)
     col_groups = jnp.arange(CROP // PHASES, dtype=jnp.int32)
     gr, gi = _cos_sin(jnp.mod(offsets[:, None] * col_groups[None, :], BLOCK), BLOCK)
-    col_op = jnp.stack([gr, -gi], axis=0)
+    col_op = jnp.concatenate([gr, -gi], axis=0)
     image = lax.dot_general(
-        col_op.reshape(2 * BLOCK, CROP // PHASES),
+        col_op,
         turned.reshape(ROWS * PHASES, 2 * BLOCK),
         (((0,), (1,)), ((), ())),
         precision=lax.Precision.HIGH,

time: 110 us -> 99.9 us (0.908)
  local copies, waits for them, and re-layouts: 10.9 us -> 4.76 us
  Pallas kernels: 33.9 us -> 31.4 us
  other arithmetic: 11.5 us -> 9.75 us
    another operation x1 -> x0, local copies, waits for them, and re-layouts: 7.36 us -> none  [channel_image(): turned = jnp.stack([turned_r, turned_i], axis=2)]
    pallas_call x1, Pallas kernels: 33.9 us -> 31.4 us  [grid_slots(): pl.pallas_call(_grid_kernel, out_shape=jax.ShapeDtypeStruct((SLOTS, 2 * B...]
    another operation x2 -> x0, other arithmetic: 1.25 us -> none  [the longest x1 1.24 us: channel_image(): turned = jnp.stack([turned_r, turned_i], axis=2)]
    slice x0 -> x1, local copies, waits for them, and re-layouts: none -> 1.21 us  [channel_image(): turned_r = summed[:, :, 0] * dr - summed[:, :, 1] * di]
where the time goes in v7:
time: 99.9 us; the launch traced here: 99.7 us
  Pallas kernels  31.4 us (31%)
  blocking collectives  24.9 us (25%)
  matrix products  12.7 us (13%)
  starting transfers between devices  11.5 us (12%)
  other arithmetic  9.75 us (10%)
  local copies, waits for them, and re-layouts  4.76 us (5%)
  waiting for transfers between devices  3.81 us (4%)
    pallas_call x1, Pallas kernels, grid_slots(): pl.pallas_call(_grid_kernel, out_shape=jax.ShapeDtypeStruct((SLOTS, 2 * B...  31.4 us
    all_to_all x1, blocking collectives, body(): lax.all_to_all(send, ('grp', 'chan'), split_axis=0, concat_axis=0, tiled=...  24.9 us
    all_to_all x1, starting transfers between devices, body(): lax.all_to_all(direct, ('grp', 'chan'), split_axis=0, concat_axis=1, tile...  11.5 us
    dot_general x1, matrix products, channel_image(): jnp.einsum('tcsk,sklv->ltcv', phase_op, rows_done, precision=lax.Precisio...  5.78 us
    dot_general x1, matrix products, channel_image(): lax.dot_general(col_op, turned.reshape(ROWS * PHASES, 2 * BLOCK), (((0,),...  4.46 us
    another operation x1, other arithmetic, channel_image(): jnp.stack([jnp.stack([ar, -ai], axis=2), jnp.stack([ai, ar], axis=2)], ax...  4.23 us
    all_to_all x1, waiting for transfers between devices, body(): lax.all_to_all(direct, ('grp', 'chan'), split_axis=0, concat_axis=1, tile...  3.81 us
    dot_general x1, matrix products, channel_image(): jnp.einsum('sclku,skuv->sclv', row_op, grids, precision=lax.Precision.HIG...  2.42 us
  transfers between devices with their start and end apart: 1, of which 1 were waited for; matrix products, arithmetic and copies ran while one was open for 9% of the time, Pallas kernels for 0%

profile of v7, /device:TPU:1, one launch (start us, length us, event | category | flops | bytes accessed | tf_op | source)
XLA Modules:
  0.0 99.7 jit_solution(9817140071391541188)
XLA Ops:
  0.0 11.5 %all-to-all-start = ((bf16[128,1,16,128]{3,2,1,0:T(8,128)(2,1)}), bf16[128,1,16,128]{3,2,1,0:T(8,128)(2,1)S(1)}, u32[]{:S(2)}, u32[]{:S(2)}) async-start(bf16[128,1,16,128]{3,2,1,0:T(8,128)(2,1)} %bitcast.91), calls=%async_computation | async-start | bytes 1048576 | tf_op jit(solution)/shard_map/all_to_all | solution.py:120
  11.5 0.7 and_select_fusion.1
  12.2 0.7 fusion.55
  12.8 0.3 sine_negate_fusion
  13.1 0.6 fusion.29
  13.9 1.3 %copy.26 = bf16[1,16,128,128]{2,3,1,0:T(8,128)(2,1)S(1)} copy(bf16[1,16,128,128]{3,2,1,0:T(8,128)(2,1)} %param.12) | data formatting | bytes 1048576 | tf_op args[3]
  16.0 1.1 %fusion.18 = (f32[16,256,1,128]{3,1,2,0:T(8,128)S(1)}, f32[16,256,1,128]{3,1,2,0:T(8,128)S(1)}, f32[16,256,1,128]{3,1,2,0:T(8,128)S(1)}) fusion(f32[256,128]{1,0:T(8,128)S(1)} %get-tuple-element.20, f32[16,256]{1,0:T(8,128)S(1)} %get-tuple-element.19, f32[256,128]{1,0:T(8,128)S(1)} %get-tuple-element.21, f32[16,256]{1,0:T(8,128)S(1)} %get-tuple-element.18), kind=kLoop, calls=%fused_computation.27 | loop fusion | flops 3670016 | bytes 6586368 | tf_op jit(solution)/shard_map/neg | solution.py:90
  17.3 4.2 %maximum_bitcast_fusion = (f32[16,1,256,2,128]{4,2,3,1,0:T(8,128)}, f32[16,1,256,2,128]{4,2,3,1,0:T(8,128)}) fusion(f32[16,256,1,128]{3,1,2,0:T(8,128)S(1)} %get-tuple-element.13, f32[16,256,1,128]{3,1,2,0:T(8,128)S(1)} %get-tuple-element.15, f32[16,256,1,128]{3,1,2,0:T(8,128)S(1)} %get-tuple-element.14), kind=kLoop, calls=%fused_computation.15 | loop fusion | flops 2097152 | bytes 14680064 | tf_op jit(solution)/shard_map/stack | solution.py:90
  21.6 3.8 %all-to-all-done = bf16[128,1,16,128]{3,2,1,0:T(8,128)(2,1)S(1)} async-done(((bf16[128,1,16,128]{3,2,1,0:T(8,128)(2,1)}), bf16[128,1,16,128]{3,2,1,0:T(8,128)(2,1)S(1)}, u32[]{:S(2)}, u32[]{:S(2)}) %all-to-all-start) | async-done | bytes 524320 | tf_op jit(solution)/shard_map/all_to_all | solution.py:120
  25.4 0.2 slice_negate_fusion
  25.6 0.3 pad_maximum_fusion.1
  25.9 0.3 copy.25
  26.2 0.3 copy.24
  26.7 31.4 %shard_map.91 = bf16[16,256,128]{2,1,0:T(8,128)(2,1)S(1)} custom-call(s32[136]{0:T(256)S(1)} %copy-done.2, s32[136]{0:T(256)S(1)} %copy-done.3, s32[136]{0:T(256)S(1)} %bitcast.84, s32[1]{0:T(128)S(6)} %copy.41.count_ref, bf16[16,128,128]{2,1,0:T(8,128)(2,1)S(1)} %bitcast.80, bf16[16,128,256]{2,1,0:T(8,128)(2,1)S(1)} %pad_maximum_fusion.w_ref, ...), custom_call_target="tpu_custom_call" | custom-call | flops 3422552064 | bytes 11534336 | tf_op jit(solution)/shard_map/pallas_call | solution.py:63
  58.1 2.4 %fusion.15 = f32[16,2,256,128,1]{3,2,1,0,4:T(8,128)S(1)} fusion(bf16[16,2,128,128,1]{3,2,1,4,0:T(8,128)(2,1)S(1)} %bitcast.81, f32[16,1,256,2,128]{4,2,3,1,0:T(8,128)S(1)} %copy-done.5, f32[16,1,256,2,128]{4,2,3,1,0:T(8,128)S(1)} %copy-done.4), kind=kOutput, calls=%fused_computation.20 | convolution fusion | flops 1612709888 | bytes 13631488 | tf_op jit(solution)/shard_map/sclku,skuv->sclv/dot_general | solution.py:91
  60.5 5.8 %fusion.12 = f32[256,32,2,128]{3,1,2,0:T(8,128)S(1)} fusion(f32[16,2,256,128,1]{3,2,1,0,4:T(8,128)S(1)} %fusion.15, f32[32,1,16,2]{0,2,3,1:T(8,128)S(1)} %get-tuple-element.17, f32[32,1,16,2]{0,2,3,1:T(8,128)S(1)} %get-tuple-element.16), kind=kOutput, calls=%fused_computation.19 | convolution fusion | flops 402655232 | bytes 12591104 | tf_op jit(solution)/shard_map/tcsk,sklv->ltcv/dot_general | solution.py:97
  66.3 1.2 %fusion.60 = (f32[256,32,1,128]{3,1,2,0:T(8,128)S(1)}, f32[256,32,1,128]{3,1,2,0:T(8,128)S(1)}) fusion(f32[256,32,2,128]{3,1,2,0:T(8,128)S(1)} %fusion.12), kind=kLoop, calls=%fused_computation.104 | loop fusion | bytes 16777216 | tf_op jit(solution)/shard_map/slice | solution.py:101
  67.6 0.9 fusion.8
  68.4 4.5 %fusion = bf16[64,8192]{1,0:T(8,128)(2,1)S(1)} fusion(f32[8192,128]{1,0:T(8,128)S(1)} %get-tuple-element.6, f32[8192,128]{1,0:T(8,128)S(1)} %get-tuple-element.5, f32[128,64]{1,0:T(8,128)S(1)} %get-tuple-element.29, f32[128,64]{1,0:T(8,128)S(1)} %get-tuple-element.30), kind=kOutput, calls=%fused_computation.1 | convolution fusion | flops 808468480 | bytes 9502720 | tf_op jit(solution)/shard_map/dot_general | solution.py:107
  72.9 0.3 copy.36
  73.2 0.6 copy.28
  73.8 24.9 %all_to_all.14 = bf16[128,16,256]{2,1,0:T(8,128)(2,1)S(1)} all-to-all(bf16[128,16,256]{2,1,0:T(8,128)(2,1)S(1)} %bitcast.87), channel_id=1, replica_groups=mesh['grp'=4,'chan'=32] {'grp','chan'}, dimensions={0} | all-to-all | bytes 2097152 | tf_op jit(solution)/shard_map/all_to_all | solution.py:132
  98.7 0.2 convert_reduce_fusion
  99.0 0.7 reshape.476
  (22 shorter events, 0.7 us)
Async XLA Ops:
  0.0 25.4 %all-to-all-start = ((bf16[128,1,16,128]{3,2,1,0:T(8,128)(2,1)}), bf16[128,1,16,128]{3,2,1,0:T(8,128)(2,1)S(1)}, u32[]{:S(2)}, u32[]{:S(2)}) async-start(bf16[128,1,16,128]{3,2,1,0:T(8,128)(2,1)} %bitcast.91), calls=%async_computation | async-start | bytes 1048576 | tf_op jit(solution)/shard_map/all_to_all | solution.py:120
  21.5 5.1 %copy-start = (bf16[1,16,128,128]{3,2,1,0:T(8,128)(2,1)S(1)}, bf16[1,16,128,128]{3,2,1,0:T(8,128)(2,1)}, u32[]{:S(2)}) copy-start(bf16[1,16,128,128]{3,2,1,0:T(8,128)(2,1)} %param.11) | copy-start | bytes 1572868
  21.5 5.1 %copy-start.1 = (s32[1,136]{1,0:T(1,128)S(1)}, s32[1,136]{1,0:T(1,128)}, u32[]{:S(2)}) copy-start(s32[1,136]{1,0:T(1,128)} %param.13) | copy-start | bytes 1636
  21.5 5.1 %copy-start.2 = (s32[136]{0:T(256)S(1)}, s32[136]{0:T(256)}, u32[]{:S(2)}) copy-start(s32[136]{0:T(256)} %constant.107.clone.ptab) | copy-start | bytes 1636
  21.5 5.1 %copy-start.3 = (s32[136]{0:T(256)S(1)}, s32[136]{0:T(256)}, u32[]{:S(2)}) copy-start(s32[136]{0:T(256)} %constant.108.clone.qtab) | copy-start | bytes 1636
  26.7 31.4 %copy-start.4 = (f32[16,1,256,2,128]{4,2,3,1,0:T(8,128)S(1)}, f32[16,1,256,2,128]{4,2,3,1,0:T(8,128)}, u32[]{:S(2)}) copy-start(f32[16,1,256,2,128]{4,2,3,1,0:T(8,128)} %get-tuple-element.9) | copy-start | bytes 12582916
  26.7 31.4 %copy-start.5 = (f32[16,1,256,2,128]{4,2,3,1,0:T(8,128)S(1)}, f32[16,1,256,2,128]{4,2,3,1,0:T(8,128)}, u32[]{:S(2)}) copy-start(f32[16,1,256,2,128]{4,2,3,1,0:T(8,128)} %get-tuple-element.10) | copy-start | bytes 12582916

commit v8 on v7

--- a/solution.py
+++ b/solution.py
@@ -23,28 +23,39 @@
 TWO_PI = 2.0 * math.pi
 
 
+PAIRS_PER_STEP = 8
+
+
 def _grid_kernel(ptab, qtab, slot_ref, count_ref, v_ref, w_ref, model_ref, ku_ref, kvt_ref, out_ref, acc_ref):
-    acc_ref[...] = jnp.zeros_like(acc_ref)
+    step = pl.program_id(0)
+
+    @pl.when(step == 0)
+    def _():
+        acc_ref[...] = jnp.zeros_like(acc_ref)
+
     count = count_ref[0]
 
-    def body(k, carry):
+    def body(i, carry):
+        k = step * PAIRS_PER_STEP + i
         p = ptab[k]
         q = qtab[k]
         slot = slot_ref[k]
         gram = jnp.dot(v_ref[p], w_ref[q], preferred_element_type=jnp.float32)
-        model = jnp.concatenate([model_ref[k, 0], model_ref[k, 1]], axis=1).astype(jnp.float32)
+        model = jnp.concatenate([model_ref[i, 0], model_ref[i, 1]], axis=1).astype(jnp.float32)
         residual = (gram * (1.0 / SAMPLES) - model).astype(jnp.bfloat16)
         half = jnp.dot(ku_ref[p], residual, preferred_element_type=jnp.float32).astype(jnp.bfloat16)
         half_rows = jnp.concatenate([half[:, :TILE], half[:, TILE:]], axis=0)
         tile = jnp.dot(half_rows, kvt_ref[q], preferred_element_type=jnp.float32)
         live = (slot < count) & (slot >= 0)
         slot_c = jnp.clip(slot, 0, SLOTS - 1)
-
         acc_ref[slot_c] += jnp.where(live, tile, 0.0)
         return carry
 
-    lax.fori_loop(0, PAIRS, body, 0, unroll=17)
-    out_ref[...] = acc_ref[...].astype(out_ref.dtype)
+    lax.fori_loop(0, PAIRS_PER_STEP, body, 0, unroll=True)
+
+    @pl.when(step == pl.num_programs(0) - 1)
+    def _():
+        out_ref[...] = acc_ref[...].astype(out_ref.dtype)
 
 
 def grid_slots(antenna_volts, model_one, kernel_u_one, kernel_v_one, slots_one, count_one):
@@ -57,16 +68,32 @@
         [tiles.transpose(0, 2, 1), swapped.reshape(TILES, TILE, 2 * SAMPLES).transpose(0, 2, 1)], axis=2
     )
     kv_turned = kernel_v_one.transpose(0, 2, 1)
-    smem = pl.BlockSpec(memory_space=pltpu.SMEM)
-    vmem = pl.BlockSpec(memory_space=pltpu.VMEM)
+    steps = PAIRS // PAIRS_PER_STEP
+
+    def whole(shape):
+        return pl.BlockSpec(shape, lambda s, *_: (0,) * len(shape))
+
     flops = PAIRS * 3 * 2 * (2 * TILE) * TILE * TILE
+    grid_spec = pltpu.PrefetchScalarGridSpec(
+        num_scalar_prefetch=4,
+        grid=(steps,),
+        in_specs=[
+            whole((TILES, TILE, 2 * SAMPLES)),
+            whole((TILES, 2 * SAMPLES, 2 * TILE)),
+            pl.BlockSpec((PAIRS_PER_STEP, 2, TILE, TILE), lambda s, *_: (s, 0, 0, 0)),
+            whole((TILES, BLOCK, TILE)),
+            whole((TILES, TILE, BLOCK)),
+        ],
+        out_specs=whole((SLOTS, 2 * BLOCK, BLOCK)),
+        scratch_shapes=[pltpu.VMEM((SLOTS, 2 * BLOCK, BLOCK), jnp.float32)],
+    )
     return pl.pallas_call(
         _grid_kernel,
         out_shape=jax.ShapeDtypeStruct((SLOTS, 2 * BLOCK, BLOCK), jnp.bfloat16),
-        in_specs=[smem, smem, smem, smem, vmem, vmem, vmem, vmem, vmem],
-        out_specs=vmem,
-        scratch_shapes=[pltpu.VMEM((SLOTS, 2 * BLOCK, BLOCK), jnp.float32)],
-        compiler_params=pltpu.CompilerParams(vmem_limit_bytes=48 * 1024 * 1024),
+        grid_spec=grid_spec,
+        compiler_params=pltpu.CompilerParams(
+            dimension_semantics=("arbitrary",), vmem_limit_bytes=48 * 1024 * 1024
+        ),
         cost_estimate=pl.CostEstimate(flops=flops, transcendentals=0, bytes_accessed=11 * 1024 * 1024),
     )(ptab, qtab, slots_one, count_one, tiles, turned, model_one, kernel_u_one, kv_turned)
 

time: 99.9 us -> 101 us (1.011)
  no operation moved by 1% of the time
where the time goes in v8:
time: 101 us
  Pallas kernels  32.4 us (32%)
  blocking collectives  24.9 us (25%)
  matrix products  12.7 us (13%)
  starting transfers between devices  11.5 us (11%)
  other arithmetic  9.75 us (10%)
  local copies, waits for them, and re-layouts  4.76 us (5%)
  waiting for transfers between devices  3.81 us (4%)
    pallas_call x1, Pallas kernels, grid_slots(): pl.pallas_call(_grid_kernel, out_shape=jax.ShapeDtypeStruct((SLOTS, 2 * B...  32.4 us
    all_to_all x1, blocking collectives, body(): lax.all_to_all(send, ('grp', 'chan'), split_axis=0, concat_axis=0, tiled=...  24.9 us
    all_to_all x1, starting transfers between devices, body(): lax.all_to_all(direct, ('grp', 'chan'), split_axis=0, concat_axis=1, tile...  11.5 us
    dot_general x1, matrix products, channel_image(): jnp.einsum('tcsk,sklv->ltcv', phase_op, rows_done, precision=lax.Precisio...  5.78 us
    dot_general x1, matrix products, channel_image(): lax.dot_general(col_op, turned.reshape(ROWS * PHASES, 2 * BLOCK), (((0,),...  4.46 us
    another operation x1, other arithmetic, channel_image(): jnp.stack([jnp.stack([ar, -ai], axis=2), jnp.stack([ai, ar], axis=2)], ax...  4.23 us
    all_to_all x1, waiting for transfers between devices, body(): lax.all_to_all(direct, ('grp', 'chan'), split_axis=0, concat_axis=1, tile...  3.81 us
    dot_general x1, matrix products, channel_image(): jnp.einsum('sclku,skuv->sclv', row_op, grids, precision=lax.Precision.HIG...  2.42 us
  transfers between devices with their start and end apart: 1, of which 1 were waited for; matrix products, arithmetic and copies ran while one was open for 9% of the time, Pallas kernels for 0%

profile of v8, /device:TPU:1, one launch (start us, length us, event | category | flops | bytes accessed | tf_op | source)
XLA Modules:
  0.0 100.7 jit_solution(7515508792172810499)
XLA Ops:
  0.0 11.5 %all-to-all-start = ((bf16[128,1,16,128]{3,2,1,0:T(8,128)(2,1)}), bf16[128,1,16,128]{3,2,1,0:T(8,128)(2,1)S(1)}, u32[]{:S(2)}, u32[]{:S(2)}) async-start(bf16[128,1,16,128]{3,2,1,0:T(8,128)(2,1)} %bitcast.91), calls=%async_computation | async-start | bytes 1048576 | tf_op jit(solution)/shard_map/all_to_all | solution.py:147
  11.5 0.7 and_select_fusion.1
  12.2 0.7 fusion.55
  12.8 0.3 sine_negate_fusion
  13.1 0.6 fusion.29
  13.9 1.3 %copy.26 = bf16[1,16,128,128]{2,3,1,0:T(8,128)(2,1)S(1)} copy(bf16[1,16,128,128]{3,2,1,0:T(8,128)(2,1)} %param.12) | data formatting | bytes 1048576 | tf_op args[3]
  16.0 1.1 %fusion.18 = (f32[16,256,1,128]{3,1,2,0:T(8,128)S(1)}, f32[16,256,1,128]{3,1,2,0:T(8,128)S(1)}, f32[16,256,1,128]{3,1,2,0:T(8,128)S(1)}) fusion(f32[256,128]{1,0:T(8,128)S(1)} %get-tuple-element.20, f32[16,256]{1,0:T(8,128)S(1)} %get-tuple-element.19, f32[256,128]{1,0:T(8,128)S(1)} %get-tuple-element.21, f32[16,256]{1,0:T(8,128)S(1)} %get-tuple-element.18), kind=kLoop, calls=%fused_computation.27 | loop fusion | flops 3670016 | bytes 6586368 | tf_op jit(solution)/shard_map/neg | solution.py:117
  17.3 4.2 %maximum_bitcast_fusion = (f32[16,1,256,2,128]{4,2,3,1,0:T(8,128)}, f32[16,1,256,2,128]{4,2,3,1,0:T(8,128)}) fusion(f32[16,256,1,128]{3,1,2,0:T(8,128)S(1)} %get-tuple-element.13, f32[16,256,1,128]{3,1,2,0:T(8,128)S(1)} %get-tuple-element.15, f32[16,256,1,128]{3,1,2,0:T(8,128)S(1)} %get-tuple-element.14), kind=kLoop, calls=%fused_computation.15 | loop fusion | flops 2097152 | bytes 14680064 | tf_op jit(solution)/shard_map/stack | solution.py:117
  21.6 3.8 %all-to-all-done = bf16[128,1,16,128]{3,2,1,0:T(8,128)(2,1)S(1)} async-done(((bf16[128,1,16,128]{3,2,1,0:T(8,128)(2,1)}), bf16[128,1,16,128]{3,2,1,0:T(8,128)(2,1)S(1)}, u32[]{:S(2)}, u32[]{:S(2)}) %all-to-all-start) | async-done | bytes 524320 | tf_op jit(solution)/shard_map/all_to_all | solution.py:147
  25.4 0.2 slice_negate_fusion
  25.6 0.3 pad_maximum_fusion.1
  25.9 0.3 copy.25
  26.2 0.3 copy.24
  26.7 32.4 %shard_map.91 = bf16[16,256,128]{2,1,0:T(8,128)(2,1)S(1)} custom-call(s32[136]{0:T(256)S(1)} %copy-done.2, s32[136]{0:T(256)S(1)} %copy-done.3, s32[136]{0:T(256)S(1)} %bitcast.84, s32[1]{0:T(128)S(6)} %copy.41.count_ref, bf16[16,128,128]{2,1,0:T(8,128)(2,1)S(1)} %bitcast.80, bf16[16,128,256]{2,1,0:T(8,128)(2,1)S(1)} %pad_maximum_fusion.w_ref, ...), custom_call_target="tpu_custom_call" | custom-call | flops 3422552064 | bytes 11534336 | tf_op jit(solution)/shard_map/pallas_call | solution.py:90
  59.1 2.4 %fusion.15 = f32[16,2,256,128,1]{3,2,1,0,4:T(8,128)S(1)} fusion(bf16[16,2,128,128,1]{3,2,1,4,0:T(8,128)(2,1)S(1)} %bitcast.81, f32[16,1,256,2,128]{4,2,3,1,0:T(8,128)S(1)} %copy-done.5, f32[16,1,256,2,128]{4,2,3,1,0:T(8,128)S(1)} %copy-done.4), kind=kOutput, calls=%fused_computation.20 | convolution fusion | flops 1612709888 | bytes 13631488 | tf_op jit(solution)/shard_map/sclku,skuv->sclv/dot_general | solution.py:118
  61.5 5.8 %fusion.12 = f32[256,32,2,128]{3,1,2,0:T(8,128)S(1)} fusion(f32[16,2,256,128,1]{3,2,1,0,4:T(8,128)S(1)} %fusion.15, f32[32,1,16,2]{0,2,3,1:T(8,128)S(1)} %get-tuple-element.17, f32[32,1,16,2]{0,2,3,1:T(8,128)S(1)} %get-tuple-element.16), kind=kOutput, calls=%fused_computation.19 | convolution fusion | flops 402655232 | bytes 12591104 | tf_op jit(solution)/shard_map/tcsk,sklv->ltcv/dot_general | solution.py:124
  67.3 1.2 %fusion.60 = (f32[256,32,1,128]{3,1,2,0:T(8,128)S(1)}, f32[256,32,1,128]{3,1,2,0:T(8,128)S(1)}) fusion(f32[256,32,2,128]{3,1,2,0:T(8,128)S(1)} %fusion.12), kind=kLoop, calls=%fused_computation.104 | loop fusion | bytes 16777216 | tf_op jit(solution)/shard_map/slice | solution.py:128
  68.5 0.9 fusion.8
  69.4 4.5 %fusion = bf16[64,8192]{1,0:T(8,128)(2,1)S(1)} fusion(f32[8192,128]{1,0:T(8,128)S(1)} %get-tuple-element.6, f32[8192,128]{1,0:T(8,128)S(1)} %get-tuple-element.5, f32[128,64]{1,0:T(8,128)S(1)} %get-tuple-element.29, f32[128,64]{1,0:T(8,128)S(1)} %get-tuple-element.30), kind=kOutput, calls=%fused_computation.1 | convolution fusion | flops 808468480 | bytes 9502720 | tf_op jit(solution)/shard_map/dot_general | solution.py:134
  73.9 0.3 copy.36
  74.1 0.6 copy.28
  74.7 24.9 %all_to_all.14 = bf16[128,16,256]{2,1,0:T(8,128)(2,1)S(1)} all-to-all(bf16[128,16,256]{2,1,0:T(8,128)(2,1)S(1)} %bitcast.87), channel_id=1, replica_groups=mesh['grp'=4,'chan'=32] {'grp','chan'}, dimensions={0} | all-to-all | bytes 2097152 | tf_op jit(solution)/shard_map/all_to_all | solution.py:159
  99.7 0.2 convert_reduce_fusion
  100.0 0.7 reshape.476
  (22 shorter events, 0.7 us)
Async XLA Ops:
  0.0 25.4 %all-to-all-start = ((bf16[128,1,16,128]{3,2,1,0:T(8,128)(2,1)}), bf16[128,1,16,128]{3,2,1,0:T(8,128)(2,1)S(1)}, u32[]{:S(2)}, u32[]{:S(2)}) async-start(bf16[128,1,16,128]{3,2,1,0:T(8,128)(2,1)} %bitcast.91), calls=%async_computation | async-start | bytes 1048576 | tf_op jit(solution)/shard_map/all_to_all | solution.py:147
  21.5 5.1 %copy-start = (bf16[1,16,128,128]{3,2,1,0:T(8,128)(2,1)S(1)}, bf16[1,16,128,128]{3,2,1,0:T(8,128)(2,1)}, u32[]{:S(2)}) copy-start(bf16[1,16,128,128]{3,2,1,0:T(8,128)(2,1)} %param.11) | copy-start | bytes 1572868
  21.5 5.1 %copy-start.1 = (s32[1,136]{1,0:T(1,128)S(1)}, s32[1,136]{1,0:T(1,128)}, u32[]{:S(2)}) copy-start(s32[1,136]{1,0:T(1,128)} %param.13) | copy-start | bytes 1636
  21.5 5.1 %copy-start.2 = (s32[136]{0:T(256)S(1)}, s32[136]{0:T(256)}, u32[]{:S(2)}) copy-start(s32[136]{0:T(256)} %constant.107.clone.ptab) | copy-start | bytes 1636
  21.5 5.1 %copy-start.3 = (s32[136]{0:T(256)S(1)}, s32[136]{0:T(256)}, u32[]{:S(2)}) copy-start(s32[136]{0:T(256)} %constant.108.clone.qtab) | copy-start | bytes 1636
  26.7 32.4 %copy-start.4 = (f32[16,1,256,2,128]{4,2,3,1,0:T(8,128)S(1)}, f32[16,1,256,2,128]{4,2,3,1,0:T(8,128)}, u32[]{:S(2)}) copy-start(f32[16,1,256,2,128]{4,2,3,1,0:T(8,128)} %get-tuple-element.9) | copy-start | bytes 12582916
  26.7 32.4 %copy-start.5 = (f32[16,1,256,2,128]{4,2,3,1,0:T(8,128)S(1)}, f32[16,1,256,2,128]{4,2,3,1,0:T(8,128)}, u32[]{:S(2)}) copy-start(f32[16,1,256,2,128]{4,2,3,1,0:T(8,128)} %get-tuple-element.10) | copy-start | bytes 12582916

commit v9 on v7

--- a/solution.py
+++ b/solution.py
@@ -43,7 +43,7 @@
         acc_ref[slot_c] += jnp.where(live, tile, 0.0)
         return carry
 
-    lax.fori_loop(0, PAIRS, body, 0, unroll=17)
+    lax.fori_loop(0, PAIRS, body, 0, unroll=34)
     out_ref[...] = acc_ref[...].astype(out_ref.dtype)
 
 

time: 99.9 us -> 98.9 us (0.990)
  Pallas kernels: 31.4 us -> 30.4 us
    pallas_call x1, Pallas kernels: 31.4 us -> 30.4 us  [grid_slots(): pl.pallas_call(_grid_kernel, out_shape=jax.ShapeDtypeStruct((SLOTS, 2 * B...]
where the time goes in v9:
time: 98.9 us; the launch traced here: 98.7 us
  Pallas kernels  30.4 us (31%)
  blocking collectives  24.9 us (25%)
  matrix products  12.7 us (13%)
  starting transfers between devices  11.5 us (12%)
  other arithmetic  9.75 us (10%)
  local copies, waits for them, and re-layouts  4.76 us (5%)
  waiting for transfers between devices  3.81 us (4%)
    pallas_call x1, Pallas kernels, grid_slots(): pl.pallas_call(_grid_kernel, out_shape=jax.ShapeDtypeStruct((SLOTS, 2 * B...  30.4 us
    all_to_all x1, blocking collectives, body(): lax.all_to_all(send, ('grp', 'chan'), split_axis=0, concat_axis=0, tiled=...  24.9 us
    all_to_all x1, starting transfers between devices, body(): lax.all_to_all(direct, ('grp', 'chan'), split_axis=0, concat_axis=1, tile...  11.5 us
    dot_general x1, matrix products, channel_image(): jnp.einsum('tcsk,sklv->ltcv', phase_op, rows_done, precision=lax.Precisio...  5.78 us
    dot_general x1, matrix products, channel_image(): lax.dot_general(col_op, turned.reshape(ROWS * PHASES, 2 * BLOCK), (((0,),...  4.46 us
    another operation x1, other arithmetic, channel_image(): jnp.stack([jnp.stack([ar, -ai], axis=2), jnp.stack([ai, ar], axis=2)], ax...  4.23 us
    all_to_all x1, waiting for transfers between devices, body(): lax.all_to_all(direct, ('grp', 'chan'), split_axis=0, concat_axis=1, tile...  3.81 us
    dot_general x1, matrix products, channel_image(): jnp.einsum('sclku,skuv->sclv', row_op, grids, precision=lax.Precision.HIG...  2.42 us
  transfers between devices with their start and end apart: 1, of which 1 were waited for; matrix products, arithmetic and copies ran while one was open for 9% of the time, Pallas kernels for 0%

profile of v9, /device:TPU:1, one launch (start us, length us, event | category | flops | bytes accessed | tf_op | source)
XLA Modules:
  0.0 98.7 jit_solution(7383048623926597358)
XLA Ops:
  0.0 11.5 %all-to-all-start = ((bf16[128,1,16,128]{3,2,1,0:T(8,128)(2,1)}), bf16[128,1,16,128]{3,2,1,0:T(8,128)(2,1)S(1)}, u32[]{:S(2)}, u32[]{:S(2)}) async-start(bf16[128,1,16,128]{3,2,1,0:T(8,128)(2,1)} %bitcast.91), calls=%async_computation | async-start | bytes 1048576 | tf_op jit(solution)/shard_map/all_to_all | solution.py:120
  11.5 0.7 and_select_fusion.1
  12.2 0.7 fusion.55
  12.8 0.3 sine_negate_fusion
  13.1 0.6 fusion.29
  13.9 1.3 %copy.26 = bf16[1,16,128,128]{2,3,1,0:T(8,128)(2,1)S(1)} copy(bf16[1,16,128,128]{3,2,1,0:T(8,128)(2,1)} %param.12) | data formatting | bytes 1048576 | tf_op args[3]
  16.0 1.1 %fusion.18 = (f32[16,256,1,128]{3,1,2,0:T(8,128)S(1)}, f32[16,256,1,128]{3,1,2,0:T(8,128)S(1)}, f32[16,256,1,128]{3,1,2,0:T(8,128)S(1)}) fusion(f32[256,128]{1,0:T(8,128)S(1)} %get-tuple-element.20, f32[16,256]{1,0:T(8,128)S(1)} %get-tuple-element.19, f32[256,128]{1,0:T(8,128)S(1)} %get-tuple-element.21, f32[16,256]{1,0:T(8,128)S(1)} %get-tuple-element.18), kind=kLoop, calls=%fused_computation.27 | loop fusion | flops 3670016 | bytes 6586368 | tf_op jit(solution)/shard_map/neg | solution.py:90
  17.3 4.2 %maximum_bitcast_fusion = (f32[16,1,256,2,128]{4,2,3,1,0:T(8,128)}, f32[16,1,256,2,128]{4,2,3,1,0:T(8,128)}) fusion(f32[16,256,1,128]{3,1,2,0:T(8,128)S(1)} %get-tuple-element.13, f32[16,256,1,128]{3,1,2,0:T(8,128)S(1)} %get-tuple-element.15, f32[16,256,1,128]{3,1,2,0:T(8,128)S(1)} %get-tuple-element.14), kind=kLoop, calls=%fused_computation.15 | loop fusion | flops 2097152 | bytes 14680064 | tf_op jit(solution)/shard_map/stack | solution.py:90
  21.6 3.8 %all-to-all-done = bf16[128,1,16,128]{3,2,1,0:T(8,128)(2,1)S(1)} async-done(((bf16[128,1,16,128]{3,2,1,0:T(8,128)(2,1)}), bf16[128,1,16,128]{3,2,1,0:T(8,128)(2,1)S(1)}, u32[]{:S(2)}, u32[]{:S(2)}) %all-to-all-start) | async-done | bytes 524320 | tf_op jit(solution)/shard_map/all_to_all | solution.py:120
  25.4 0.2 slice_negate_fusion
  25.6 0.3 pad_maximum_fusion.1
  25.9 0.3 copy.25
  26.2 0.3 copy.24
  26.7 30.4 %shard_map.91 = bf16[16,256,128]{2,1,0:T(8,128)(2,1)S(1)} custom-call(s32[136]{0:T(256)S(1)} %copy-done.2, s32[136]{0:T(256)S(1)} %copy-done.3, s32[136]{0:T(256)S(1)} %bitcast.84, s32[1]{0:T(128)S(6)} %copy.41.count_ref, bf16[16,128,128]{2,1,0:T(8,128)(2,1)S(1)} %bitcast.80, bf16[16,128,256]{2,1,0:T(8,128)(2,1)S(1)} %pad_maximum_fusion.w_ref, ...), custom_call_target="tpu_custom_call" | custom-call | flops 3422552064 | bytes 11534336 | tf_op jit(solution)/shard_map/pallas_call | solution.py:63
  57.1 2.4 %fusion.15 = f32[16,2,256,128,1]{3,2,1,0,4:T(8,128)S(1)} fusion(bf16[16,2,128,128,1]{3,2,1,4,0:T(8,128)(2,1)S(1)} %bitcast.81, f32[16,1,256,2,128]{4,2,3,1,0:T(8,128)S(1)} %copy-done.5, f32[16,1,256,2,128]{4,2,3,1,0:T(8,128)S(1)} %copy-done.4), kind=kOutput, calls=%fused_computation.20 | convolution fusion | flops 1612709888 | bytes 13631488 | tf_op jit(solution)/shard_map/sclku,skuv->sclv/dot_general | solution.py:91
  59.5 5.8 %fusion.12 = f32[256,32,2,128]{3,1,2,0:T(8,128)S(1)} fusion(f32[16,2,256,128,1]{3,2,1,0,4:T(8,128)S(1)} %fusion.15, f32[32,1,16,2]{0,2,3,1:T(8,128)S(1)} %get-tuple-element.17, f32[32,1,16,2]{0,2,3,1:T(8,128)S(1)} %get-tuple-element.16), kind=kOutput, calls=%fused_computation.19 | convolution fusion | flops 402655232 | bytes 12591104 | tf_op jit(solution)/shard_map/tcsk,sklv->ltcv/dot_general | solution.py:97
  65.3 1.2 %fusion.60 = (f32[256,32,1,128]{3,1,2,0:T(8,128)S(1)}, f32[256,32,1,128]{3,1,2,0:T(8,128)S(1)}) fusion(f32[256,32,2,128]{3,1,2,0:T(8,128)S(1)} %fusion.12), kind=kLoop, calls=%fused_computation.104 | loop fusion | bytes 16777216 | tf_op jit(solution)/shard_map/slice | solution.py:101
  66.5 0.9 fusion.8
  67.4 4.5 %fusion = bf16[64,8192]{1,0:T(8,128)(2,1)S(1)} fusion(f32[8192,128]{1,0:T(8,128)S(1)} %get-tuple-element.6, f32[8192,128]{1,0:T(8,128)S(1)} %get-tuple-element.5, f32[128,64]{1,0:T(8,128)S(1)} %get-tuple-element.29, f32[128,64]{1,0:T(8,128)S(1)} %get-tuple-element.30), kind=kOutput, calls=%fused_computation.1 | convolution fusion | flops 808468480 | bytes 9502720 | tf_op jit(solution)/shard_map/dot_general | solution.py:107
  71.9 0.3 copy.36
  72.2 0.6 copy.28
  72.7 24.9 %all_to_all.14 = bf16[128,16,256]{2,1,0:T(8,128)(2,1)S(1)} all-to-all(bf16[128,16,256]{2,1,0:T(8,128)(2,1)S(1)} %bitcast.87), channel_id=1, replica_groups=mesh['grp'=4,'chan'=32] {'grp','chan'}, dimensions={0} | all-to-all | bytes 2097152 | tf_op jit(solution)/shard_map/all_to_all | solution.py:132
  97.7 0.2 convert_reduce_fusion
  98.0 0.7 reshape.476
  (22 shorter events, 0.7 us)
Async XLA Ops:
  0.0 25.4 %all-to-all-start = ((bf16[128,1,16,128]{3,2,1,0:T(8,128)(2,1)}), bf16[128,1,16,128]{3,2,1,0:T(8,128)(2,1)S(1)}, u32[]{:S(2)}, u32[]{:S(2)}) async-start(bf16[128,1,16,128]{3,2,1,0:T(8,128)(2,1)} %bitcast.91), calls=%async_computation | async-start | bytes 1048576 | tf_op jit(solution)/shard_map/all_to_all | solution.py:120
  21.5 5.1 %copy-start = (bf16[1,16,128,128]{3,2,1,0:T(8,128)(2,1)S(1)}, bf16[1,16,128,128]{3,2,1,0:T(8,128)(2,1)}, u32[]{:S(2)}) copy-start(bf16[1,16,128,128]{3,2,1,0:T(8,128)(2,1)} %param.11) | copy-start | bytes 1572868
  21.5 5.1 %copy-start.1 = (s32[1,136]{1,0:T(1,128)S(1)}, s32[1,136]{1,0:T(1,128)}, u32[]{:S(2)}) copy-start(s32[1,136]{1,0:T(1,128)} %param.13) | copy-start | bytes 1636
  21.5 5.1 %copy-start.2 = (s32[136]{0:T(256)S(1)}, s32[136]{0:T(256)}, u32[]{:S(2)}) copy-start(s32[136]{0:T(256)} %constant.107.clone.ptab) | copy-start | bytes 1636
  21.5 5.1 %copy-start.3 = (s32[136]{0:T(256)S(1)}, s32[136]{0:T(256)}, u32[]{:S(2)}) copy-start(s32[136]{0:T(256)} %constant.108.clone.qtab) | copy-start | bytes 1636
  26.7 30.4 %copy-start.4 = (f32[16,1,256,2,128]{4,2,3,1,0:T(8,128)S(1)}, f32[16,1,256,2,128]{4,2,3,1,0:T(8,128)}, u32[]{:S(2)}) copy-start(f32[16,1,256,2,128]{4,2,3,1,0:T(8,128)} %get-tuple-element.9) | copy-start | bytes 12582916
  26.7 30.4 %copy-start.5 = (f32[16,1,256,2,128]{4,2,3,1,0:T(8,128)S(1)}, f32[16,1,256,2,128]{4,2,3,1,0:T(8,128)}, u32[]{:S(2)}) copy-start(f32[16,1,256,2,128]{4,2,3,1,0:T(8,128)} %get-tuple-element.10) | copy-start | bytes 12582916

commit v10 on v9

--- a/solution.py
+++ b/solution.py
@@ -43,7 +43,7 @@
         acc_ref[slot_c] += jnp.where(live, tile, 0.0)
         return carry
 
-    lax.fori_loop(0, PAIRS, body, 0, unroll=34)
+    lax.fori_loop(0, PAIRS, body, 0, unroll=68)
     out_ref[...] = acc_ref[...].astype(out_ref.dtype)
 
 

time: 98.9 us -> 98.6 us (level)
  no operation moved by 1% of the time
where the time goes in v10:
time: 98.6 us; the launch traced here: 98.4 us
  Pallas kernels  30.1 us (31%)
  blocking collectives  24.9 us (25%)
  matrix products  12.7 us (13%)
  starting transfers between devices  11.5 us (12%)
  other arithmetic  9.75 us (10%)
  local copies, waits for them, and re-layouts  4.76 us (5%)
  waiting for transfers between devices  3.81 us (4%)
    pallas_call x1, Pallas kernels, grid_slots(): pl.pallas_call(_grid_kernel, out_shape=jax.ShapeDtypeStruct((SLOTS, 2 * B...  30.1 us
    all_to_all x1, blocking collectives, body(): lax.all_to_all(send, ('grp', 'chan'), split_axis=0, concat_axis=0, tiled=...  24.9 us
    all_to_all x1, starting transfers between devices, body(): lax.all_to_all(direct, ('grp', 'chan'), split_axis=0, concat_axis=1, tile...  11.5 us
    dot_general x1, matrix products, channel_image(): jnp.einsum('tcsk,sklv->ltcv', phase_op, rows_done, precision=lax.Precisio...  5.79 us
    dot_general x1, matrix products, channel_image(): lax.dot_general(col_op, turned.reshape(ROWS * PHASES, 2 * BLOCK), (((0,),...  4.5 us
    another operation x1, other arithmetic, channel_image(): jnp.stack([jnp.stack([ar, -ai], axis=2), jnp.stack([ai, ar], axis=2)], ax...  4.23 us
    all_to_all x1, waiting for transfers between devices, body(): lax.all_to_all(direct, ('grp', 'chan'), split_axis=0, concat_axis=1, tile...  3.81 us
    dot_general x1, matrix products, channel_image(): jnp.einsum('sclku,skuv->sclv', row_op, grids, precision=lax.Precision.HIG...  2.42 us
  transfers between devices with their start and end apart: 1, of which 1 were waited for; matrix products, arithmetic and copies ran while one was open for 9% of the time, Pallas kernels for 0%

profile of v10, /device:TPU:1, one launch (start us, length us, event | category | flops | bytes accessed | tf_op | source)
XLA Modules:
  0.0 98.4 jit_solution(14017712367747231307)
XLA Ops:
  0.0 11.5 %all-to-all-start = ((bf16[128,1,16,128]{3,2,1,0:T(8,128)(2,1)}), bf16[128,1,16,128]{3,2,1,0:T(8,128)(2,1)S(1)}, u32[]{:S(2)}, u32[]{:S(2)}) async-start(bf16[128,1,16,128]{3,2,1,0:T(8,128)(2,1)} %bitcast.91), calls=%async_computation | async-start | bytes 1048576 | tf_op jit(solution)/shard_map/all_to_all | solution.py:120
  11.5 0.7 and_select_fusion.1
  12.2 0.7 fusion.55
  12.8 0.3 sine_negate_fusion
  13.1 0.6 fusion.29
  13.9 1.3 %copy.26 = bf16[1,16,128,128]{2,3,1,0:T(8,128)(2,1)S(1)} copy(bf16[1,16,128,128]{3,2,1,0:T(8,128)(2,1)} %param.12) | data formatting | bytes 1048576 | tf_op args[3]
  16.0 1.1 %fusion.18 = (f32[16,256,1,128]{3,1,2,0:T(8,128)S(1)}, f32[16,256,1,128]{3,1,2,0:T(8,128)S(1)}, f32[16,256,1,128]{3,1,2,0:T(8,128)S(1)}) fusion(f32[256,128]{1,0:T(8,128)S(1)} %get-tuple-element.20, f32[16,256]{1,0:T(8,128)S(1)} %get-tuple-element.19, f32[256,128]{1,0:T(8,128)S(1)} %get-tuple-element.21, f32[16,256]{1,0:T(8,128)S(1)} %get-tuple-element.18), kind=kLoop, calls=%fused_computation.27 | loop fusion | flops 3670016 | bytes 6586368 | tf_op jit(solution)/shard_map/neg | solution.py:90
  17.3 4.2 %maximum_bitcast_fusion = (f32[16,1,256,2,128]{4,2,3,1,0:T(8,128)}, f32[16,1,256,2,128]{4,2,3,1,0:T(8,128)}) fusion(f32[16,256,1,128]{3,1,2,0:T(8,128)S(1)} %get-tuple-element.13, f32[16,256,1,128]{3,1,2,0:T(8,128)S(1)} %get-tuple-element.15, f32[16,256,1,128]{3,1,2,0:T(8,128)S(1)} %get-tuple-element.14), kind=kLoop, calls=%fused_computation.15 | loop fusion | flops 2097152 | bytes 14680064 | tf_op jit(solution)/shard_map/stack | solution.py:90
  21.6 3.8 %all-to-all-done = bf16[128,1,16,128]{3,2,1,0:T(8,128)(2,1)S(1)} async-done(((bf16[128,1,16,128]{3,2,1,0:T(8,128)(2,1)}), bf16[128,1,16,128]{3,2,1,0:T(8,128)(2,1)S(1)}, u32[]{:S(2)}, u32[]{:S(2)}) %all-to-all-start) | async-done | bytes 524320 | tf_op jit(solution)/shard_map/all_to_all | solution.py:120
  25.4 0.2 slice_negate_fusion
  25.6 0.3 pad_maximum_fusion.1
  25.9 0.3 copy.25
  26.2 0.3 copy.24
  26.7 30.1 %shard_map.91 = bf16[16,256,128]{2,1,0:T(8,128)(2,1)S(1)} custom-call(s32[136]{0:T(256)S(1)} %copy-done.2, s32[136]{0:T(256)S(1)} %copy-done.3, s32[136]{0:T(256)S(1)} %bitcast.84, s32[1]{0:T(128)S(6)} %copy.41.count_ref, bf16[16,128,128]{2,1,0:T(8,128)(2,1)S(1)} %bitcast.80, bf16[16,128,256]{2,1,0:T(8,128)(2,1)S(1)} %pad_maximum_fusion.w_ref, ...), custom_call_target="tpu_custom_call" | custom-call | flops 3422552064 | bytes 11534336 | tf_op jit(solution)/shard_map/pallas_call | solution.py:63
  56.8 2.4 %fusion.15 = f32[16,2,256,128,1]{3,2,1,0,4:T(8,128)S(1)} fusion(bf16[16,2,128,128,1]{3,2,1,4,0:T(8,128)(2,1)S(1)} %bitcast.81, f32[16,1,256,2,128]{4,2,3,1,0:T(8,128)S(1)} %copy-done.5, f32[16,1,256,2,128]{4,2,3,1,0:T(8,128)S(1)} %copy-done.4), kind=kOutput, calls=%fused_computation.20 | convolution fusion | flops 1612709888 | bytes 13631488 | tf_op jit(solution)/shard_map/sclku,skuv->sclv/dot_general | solution.py:91
  59.2 5.8 %fusion.12 = f32[256,32,2,128]{3,1,2,0:T(8,128)S(1)} fusion(f32[16,2,256,128,1]{3,2,1,0,4:T(8,128)S(1)} %fusion.15, f32[32,1,16,2]{0,2,3,1:T(8,128)S(1)} %get-tuple-element.17, f32[32,1,16,2]{0,2,3,1:T(8,128)S(1)} %get-tuple-element.16), kind=kOutput, calls=%fused_computation.19 | convolution fusion | flops 402655232 | bytes 12591104 | tf_op jit(solution)/shard_map/tcsk,sklv->ltcv/dot_general | solution.py:97
  65.0 1.2 %fusion.60 = (f32[256,32,1,128]{3,1,2,0:T(8,128)S(1)}, f32[256,32,1,128]{3,1,2,0:T(8,128)S(1)}) fusion(f32[256,32,2,128]{3,1,2,0:T(8,128)S(1)} %fusion.12), kind=kLoop, calls=%fused_computation.104 | loop fusion | bytes 16777216 | tf_op jit(solution)/shard_map/slice | solution.py:101
  66.2 0.9 fusion.8
  67.1 4.5 %fusion = bf16[64,8192]{1,0:T(8,128)(2,1)S(1)} fusion(f32[8192,128]{1,0:T(8,128)S(1)} %get-tuple-element.6, f32[8192,128]{1,0:T(8,128)S(1)} %get-tuple-element.5, f32[128,64]{1,0:T(8,128)S(1)} %get-tuple-element.29, f32[128,64]{1,0:T(8,128)S(1)} %get-tuple-element.30), kind=kOutput, calls=%fused_computation.1 | convolution fusion | flops 808468480 | bytes 9502720 | tf_op jit(solution)/shard_map/dot_general | solution.py:107
  71.6 0.3 copy.36
  71.9 0.6 copy.28
  72.5 24.9 %all_to_all.14 = bf16[128,16,256]{2,1,0:T(8,128)(2,1)S(1)} all-to-all(bf16[128,16,256]{2,1,0:T(8,128)(2,1)S(1)} %bitcast.87), channel_id=1, replica_groups=mesh['grp'=4,'chan'=32] {'grp','chan'}, dimensions={0} | all-to-all | bytes 2097152 | tf_op jit(solution)/shard_map/all_to_all | solution.py:132
  97.4 0.2 convert_reduce_fusion
  97.7 0.7 reshape.476
  (22 shorter events, 0.7 us)
Async XLA Ops:
  0.0 25.4 %all-to-all-start = ((bf16[128,1,16,128]{3,2,1,0:T(8,128)(2,1)}), bf16[128,1,16,128]{3,2,1,0:T(8,128)(2,1)S(1)}, u32[]{:S(2)}, u32[]{:S(2)}) async-start(bf16[128,1,16,128]{3,2,1,0:T(8,128)(2,1)} %bitcast.91), calls=%async_computation | async-start | bytes 1048576 | tf_op jit(solution)/shard_map/all_to_all | solution.py:120
  21.5 5.1 %copy-start = (bf16[1,16,128,128]{3,2,1,0:T(8,128)(2,1)S(1)}, bf16[1,16,128,128]{3,2,1,0:T(8,128)(2,1)}, u32[]{:S(2)}) copy-start(bf16[1,16,128,128]{3,2,1,0:T(8,128)(2,1)} %param.11) | copy-start | bytes 1572868
  21.5 5.1 %copy-start.1 = (s32[1,136]{1,0:T(1,128)S(1)}, s32[1,136]{1,0:T(1,128)}, u32[]{:S(2)}) copy-start(s32[1,136]{1,0:T(1,128)} %param.13) | copy-start | bytes 1636
  21.5 5.1 %copy-start.2 = (s32[136]{0:T(256)S(1)}, s32[136]{0:T(256)}, u32[]{:S(2)}) copy-start(s32[136]{0:T(256)} %constant.107.clone.ptab) | copy-start | bytes 1636
  21.5 5.1 %copy-start.3 = (s32[136]{0:T(256)S(1)}, s32[136]{0:T(256)}, u32[]{:S(2)}) copy-start(s32[136]{0:T(256)} %constant.108.clone.qtab) | copy-start | bytes 1636
  26.7 30.1 %copy-start.4 = (f32[16,1,256,2,128]{4,2,3,1,0:T(8,128)S(1)}, f32[16,1,256,2,128]{4,2,3,1,0:T(8,128)}, u32[]{:S(2)}) copy-start(f32[16,1,256,2,128]{4,2,3,1,0:T(8,128)} %get-tuple-element.9) | copy-start | bytes 12582916
  26.7 30.1 %copy-start.5 = (f32[16,1,256,2,128]{4,2,3,1,0:T(8,128)S(1)}, f32[16,1,256,2,128]{4,2,3,1,0:T(8,128)}, u32[]{:S(2)}) copy-start(f32[16,1,256,2,128]{4,2,3,1,0:T(8,128)} %get-tuple-element.10) | copy-start | bytes 12582916

commit v11 on v10

--- a/solution.py
+++ b/solution.py
@@ -78,7 +78,7 @@
 
 def channel_image(slot_grids, blocks_here):
     per_side = GRID // BLOCK
-    grids = slot_grids.reshape(SLOTS, 2, BLOCK, BLOCK).astype(jnp.float32)
+    grids = slot_grids.reshape(SLOTS, 2, BLOCK, BLOCK)
     block_rows = blocks_here // per_side
     block_cols = blocks_here % per_side
     offsets = jnp.arange(BLOCK, dtype=jnp.int32)
@@ -88,8 +88,10 @@
     ar = er[:, :, None] * br0[None] - ei[:, :, None] * bi0[None]
     ai = er[:, :, None] * bi0[None] + ei[:, :, None] * br0[None]
     row_op = jnp.stack([jnp.stack([ar, -ai], axis=2), jnp.stack([ai, ar], axis=2)], axis=1)
-    rows_done = jnp.einsum(
-        "sclku,skuv->sclv", row_op, grids, precision=lax.Precision.HIGH, preferred_element_type=jnp.float32
+    row_hi = row_op.astype(jnp.bfloat16)
+    row_lo = (row_op - row_hi.astype(jnp.float32)).astype(jnp.bfloat16)
+    rows_done = jnp.einsum("sclku,skuv->sclv", row_hi, grids, preferred_element_type=jnp.float32) + jnp.einsum(
+        "sclku,skuv->sclv", row_lo, grids, preferred_element_type=jnp.float32
     )
     phases = jnp.arange(PHASES, dtype=jnp.int32)
     zr, zi = _cos_sin(jnp.mod(phases[:, None] * block_cols[None, :], PHASES), PHASES)

time: 98.6 us -> 98.8 us (level)
    dot_general x1 -> x2, matrix products: 2.42 us -> 2.61 us  [the longest x1 1.36 us: channel_image(): jnp.einsum('sclku,skuv->sclv', row_hi, grids, preferred_element_type=jnp....]
where the time goes in v11:
time: 98.8 us; the launch traced here: 98.6 us
  Pallas kernels  30.1 us (30%)
  blocking collectives  24.9 us (25%)
  matrix products  12.9 us (13%)
  starting transfers between devices  11.5 us (12%)
  other arithmetic  9.75 us (10%)
  local copies, waits for them, and re-layouts  4.76 us (5%)
  waiting for transfers between devices  3.81 us (4%)
    pallas_call x1, Pallas kernels, grid_slots(): pl.pallas_call(_grid_kernel, out_shape=jax.ShapeDtypeStruct((SLOTS, 2 * B...  30.1 us
    all_to_all x1, blocking collectives, body(): lax.all_to_all(send, ('grp', 'chan'), split_axis=0, concat_axis=0, tiled=...  24.9 us
    all_to_all x1, starting transfers between devices, body(): lax.all_to_all(direct, ('grp', 'chan'), split_axis=0, concat_axis=1, tile...  11.5 us
    dot_general x1, matrix products, channel_image(): jnp.einsum('tcsk,sklv->ltcv', phase_op, rows_done, precision=lax.Precisio...  5.78 us
    dot_general x1, matrix products, channel_image(): lax.dot_general(col_op, turned.reshape(ROWS * PHASES, 2 * BLOCK), (((0,),...  4.49 us
    another operation x1, other arithmetic, channel_image(): jnp.stack([jnp.stack([ar, -ai], axis=2), jnp.stack([ai, ar], axis=2)], ax...  4.23 us
    all_to_all x1, waiting for transfers between devices, body(): lax.all_to_all(direct, ('grp', 'chan'), split_axis=0, concat_axis=1, tile...  3.81 us
  transfers between devices with their start and end apart: 1, of which 1 were waited for; matrix products, arithmetic and copies ran while one was open for 9% of the time, Pallas kernels for 0%

profile of v11, /device:TPU:1, one launch (start us, length us, event | category | flops | bytes accessed | tf_op | source)
XLA Modules:
  0.0 98.6 jit_solution(5491862154735344127)
XLA Ops:
  0.0 11.5 %all-to-all-start = ((bf16[128,1,16,128]{3,2,1,0:T(8,128)(2,1)}), bf16[128,1,16,128]{3,2,1,0:T(8,128)(2,1)S(1)}, u32[]{:S(2)}, u32[]{:S(2)}) async-start(bf16[128,1,16,128]{3,2,1,0:T(8,128)(2,1)} %bitcast.98), calls=%async_computation | async-start | bytes 1048576 | tf_op jit(solution)/shard_map/all_to_all | solution.py:122
  11.5 0.7 and_select_fusion.1
  12.2 0.7 fusion.55
  12.8 0.3 sine_negate_fusion
  13.1 0.6 fusion.29
  13.9 1.3 %copy.26 = bf16[1,16,128,128]{2,3,1,0:T(8,128)(2,1)S(1)} copy(bf16[1,16,128,128]{3,2,1,0:T(8,128)(2,1)} %param.12) | data formatting | bytes 1048576 | tf_op args[3]
  16.0 1.1 %fusion.18 = (f32[16,256,1,128]{3,1,2,0:T(8,128)S(1)}, f32[16,256,1,128]{3,1,2,0:T(8,128)S(1)}, f32[16,256,1,128]{3,1,2,0:T(8,128)S(1)}) fusion(f32[256,128]{1,0:T(8,128)S(1)} %get-tuple-element.20, f32[16,256]{1,0:T(8,128)S(1)} %get-tuple-element.19, f32[256,128]{1,0:T(8,128)S(1)} %get-tuple-element.21, f32[16,256]{1,0:T(8,128)S(1)} %get-tuple-element.18), kind=kLoop, calls=%fused_computation.29 | loop fusion | flops 3670016 | bytes 6586368 | tf_op jit(solution)/shard_map/neg | solution.py:90
  17.3 4.2 %maximum_bitcast_fusion = (f32[16,1,256,2,128]{4,2,3,1,0:T(8,128)}, f32[16,1,256,2,128]{4,2,3,1,0:T(8,128)}) fusion(f32[16,256,1,128]{3,1,2,0:T(8,128)S(1)} %get-tuple-element.13, f32[16,256,1,128]{3,1,2,0:T(8,128)S(1)} %get-tuple-element.15, f32[16,256,1,128]{3,1,2,0:T(8,128)S(1)} %get-tuple-element.14), kind=kLoop, calls=%fused_computation.15 | loop fusion | flops 2097152 | bytes 14680064 | tf_op jit(solution)/shard_map/stack | solution.py:90
  21.6 3.8 %all-to-all-done = bf16[128,1,16,128]{3,2,1,0:T(8,128)(2,1)S(1)} async-done(((bf16[128,1,16,128]{3,2,1,0:T(8,128)(2,1)}), bf16[128,1,16,128]{3,2,1,0:T(8,128)(2,1)S(1)}, u32[]{:S(2)}, u32[]{:S(2)}) %all-to-all-start) | async-done | bytes 524320 | tf_op jit(solution)/shard_map/all_to_all | solution.py:122
  25.4 0.2 slice_negate_fusion
  25.6 0.3 pad_maximum_fusion.2
  25.9 0.3 copy.25
  26.2 0.3 copy.24
  26.7 30.1 %shard_map.91 = bf16[16,256,128]{2,1,0:T(8,128)(2,1)S(1)} custom-call(s32[136]{0:T(256)S(1)} %copy-done.2, s32[136]{0:T(256)S(1)} %copy-done.3, s32[136]{0:T(256)S(1)} %bitcast.91, s32[1]{0:T(128)S(6)} %copy.42.count_ref, bf16[16,128,128]{2,1,0:T(8,128)(2,1)S(1)} %bitcast.86, bf16[16,128,256]{2,1,0:T(8,128)(2,1)S(1)} %pad_maximum_fusion.1.w_ref, ...), custom_call_target="tpu_custom_call" | custom-call | flops 3422552064 | bytes 11534336 | tf_op jit(solution)/shard_map/pallas_call | solution.py:63
  56.8 1.3 %fusion.12 = f32[16,2,256,128,1]{3,2,4,1,0:T(8,128)S(1)} fusion(bf16[16,2,128,128,1]{3,2,1,4,0:T(8,128)(2,1)S(1)} %bitcast.87, f32[16,1,256,2,128]{4,2,3,1,0:T(8,128)S(1)} %copy-done.5, f32[16,1,256,2,128]{4,2,3,1,0:T(8,128)S(1)} %copy-done.4), kind=kOutput, calls=%fused_computation.21 | convolution fusion | flops 547356672 | bytes 13631488 | tf_op jit(solution)/shard_map/sclku,skuv->sclv/dot_general | solution.py:93
  58.0 1.4 %fusion.11 = f32[16,2,256,128,1]{3,2,1,0,4:T(8,128)S(1)} fusion(f32[16,2,256,128,1]{3,2,4,1,0:T(8,128)S(1)} %fusion.12, bf16[16,2,128,128,1]{3,2,1,4,0:T(8,128)(2,1)S(1)} %bitcast.88, f32[16,1,256,2,128]{4,2,3,1,0:T(8,128)S(1)} %copy-done.5, f32[16,1,256,2,128]{4,2,3,1,0:T(8,128)S(1)} %copy-done.4), kind=kOutput, calls=%fused_computation.20 | convolution fusion | flops 540016640 | bytes 17825792 | tf_op jit(solution)/shard_map/sclku,skuv->sclv/dot_general | solution.py:93
  59.4 5.8 %fusion.13 = f32[256,32,2,128]{3,1,2,0:T(8,128)S(1)} fusion(f32[16,2,256,128,1]{3,2,1,0,4:T(8,128)S(1)} %fusion.11, f32[32,1,16,2]{0,2,3,1:T(8,128)S(1)} %get-tuple-element.17, f32[32,1,16,2]{0,2,3,1:T(8,128)S(1)} %get-tuple-element.16), kind=kOutput, calls=%fused_computation.22 | convolution fusion | flops 402655232 | bytes 12591104 | tf_op jit(solution)/shard_map/tcsk,sklv->ltcv/dot_general | solution.py:99
  65.2 1.2 %fusion.61 = (f32[256,32,1,128]{3,1,2,0:T(8,128)S(1)}, f32[256,32,1,128]{3,1,2,0:T(8,128)S(1)}) fusion(f32[256,32,2,128]{3,1,2,0:T(8,128)S(1)} %fusion.13), kind=kLoop, calls=%fused_computation.107 | loop fusion | bytes 16777216 | tf_op jit(solution)/shard_map/slice | solution.py:103
  66.4 0.9 fusion.7
  67.3 4.5 %fusion = bf16[64,8192]{1,0:T(8,128)(2,1)S(1)} fusion(f32[8192,128]{1,0:T(8,128)S(1)} %get-tuple-element.6, f32[8192,128]{1,0:T(8,128)S(1)} %get-tuple-element.5, f32[128,64]{1,0:T(8,128)S(1)} %get-tuple-element.29, f32[128,64]{1,0:T(8,128)S(1)} %get-tuple-element.30), kind=kOutput, calls=%fused_computation.1 | convolution fusion | flops 808468480 | bytes 9502720 | tf_op jit(solution)/shard_map/dot_general | solution.py:109
  71.8 0.3 copy.37
  72.0 0.6 copy.28
  72.6 24.9 %all_to_all.14 = bf16[128,16,256]{2,1,0:T(8,128)(2,1)S(1)} all-to-all(bf16[128,16,256]{2,1,0:T(8,128)(2,1)S(1)} %bitcast.94), channel_id=1, replica_groups=mesh['grp'=4,'chan'=32] {'grp','chan'}, dimensions={0} | all-to-all | bytes 2097152 | tf_op jit(solution)/shard_map/all_to_all | solution.py:134
  97.9 0.7 reshape.476
  (23 shorter events, 0.9 us)
Async XLA Ops:
  0.0 25.4 %all-to-all-start = ((bf16[128,1,16,128]{3,2,1,0:T(8,128)(2,1)}), bf16[128,1,16,128]{3,2,1,0:T(8,128)(2,1)S(1)}, u32[]{:S(2)}, u32[]{:S(2)}) async-start(bf16[128,1,16,128]{3,2,1,0:T(8,128)(2,1)} %bitcast.98), calls=%async_computation | async-start | bytes 1048576 | tf_op jit(solution)/shard_map/all_to_all | solution.py:122
  21.5 5.1 %copy-start = (bf16[1,16,128,128]{3,2,1,0:T(8,128)(2,1)S(1)}, bf16[1,16,128,128]{3,2,1,0:T(8,128)(2,1)}, u32[]{:S(2)}) copy-start(bf16[1,16,128,128]{3,2,1,0:T(8,128)(2,1)} %param.11) | copy-start | bytes 1572868
  21.5 5.1 %copy-start.1 = (s32[1,136]{1,0:T(1,128)S(1)}, s32[1,136]{1,0:T(1,128)}, u32[]{:S(2)}) copy-start(s32[1,136]{1,0:T(1,128)} %param.13) | copy-start | bytes 1636
  21.5 5.1 %copy-start.2 = (s32[136]{0:T(256)S(1)}, s32[136]{0:T(256)}, u32[]{:S(2)}) copy-start(s32[136]{0:T(256)} %constant.107.clone.ptab) | copy-start | bytes 1636
  21.5 5.1 %copy-start.3 = (s32[136]{0:T(256)S(1)}, s32[136]{0:T(256)}, u32[]{:S(2)}) copy-start(s32[136]{0:T(256)} %constant.108.clone.qtab) | copy-start | bytes 1636
  26.7 30.1 %copy-start.4 = (f32[16,1,256,2,128]{4,2,3,1,0:T(8,128)S(1)}, f32[16,1,256,2,128]{4,2,3,1,0:T(8,128)}, u32[]{:S(2)}) copy-start(f32[16,1,256,2,128]{4,2,3,1,0:T(8,128)} %get-tuple-element.9) | copy-start | bytes 12582916
  26.7 30.1 %copy-start.5 = (f32[16,1,256,2,128]{4,2,3,1,0:T(8,128)S(1)}, f32[16,1,256,2,128]{4,2,3,1,0:T(8,128)}, u32[]{:S(2)}) copy-start(f32[16,1,256,2,128]{4,2,3,1,0:T(8,128)} %get-tuple-element.10) | copy-start | bytes 12582916
